TPU v7x, 256 devices: a whole 4x4x8 slice. The times are simulated.
256 devices in a mesh: segment: 4 (over x), dp: 64 (over z, y, core).
Axes of the slice: x: 4, y: 4, z: 8, core: 2. Of those that a mesh axis runs over, the one named last changes fastest.
Arguments:
- x_saved: bfloat16 [4, 8192, 1536], P('segment', 'dp'), may hold values from -6 to 6
- gains: float32 [4, 1536], P('segment'), may hold values from 0.1 to 1.9
- w_in: bfloat16 [4, 1536, 3072], P('segment', 'dp'), may hold values from -0.15625 to 0.15625
- w_out: bfloat16 [4, 3072, 1536], P('segment', None, 'dp'), may hold values from -0.109375 to 0.109375
- cotangent: bfloat16 [8192, 1536], P('dp'), may hold values from -6 to 6
- lengths: int32 [64], replicated, may hold values from 1 to 256, 8192 in all
Outputs:
- grads: bfloat16 [4, 8192, 1536], P('segment', 'dp')
- gain_grads: float32 [4, 1536], P('segment')
All inputs are finite; a program needn't handle non-finite values.
Results may differ from a plain program's by a relative error of at most 0.0075.
Values may be sent and summed in bfloat16 or wider, within the bound.
No kernel may reach another device: no remote copies, remote signals or barrier semaphores. Data moves between devices by JAX's collectives and lax.ppermute only.
A program may use at most 128 MiB of HBM per device.

v0:
```python
import jax
import jax.numpy as jnp
from jax import lax
from jax.sharding import PartitionSpec as P


def passed_along(x, axis, by):
    length = lax.axis_size(axis)
    pairs = [(i, i + by) for i in range(length) if 0 <= i + by < length]
    return lax.ppermute(x, axis, pairs)


def on_device(x_saved, gains, w_in, w_out, cotangent, lengths):
    rows = cotangent.shape[0]
    width = cotangent.shape[1]
    ends = jnp.cumsum(lengths)
    position = lax.axis_index("dp") * rows + jnp.arange(rows, dtype=jnp.int32)
    utter_hit = (position[:, None] >= ends[None, :]).astype(jnp.int32)
    utter = jnp.sum(utter_hit, 1)
    onehot = (utter[:, None] == jnp.arange(lengths.shape[0], dtype=jnp.int32)[None, :]).astype(
        jnp.int32
    )
    tok_len = jnp.sum(onehot * lengths[None, :], 1).astype(jnp.float32)
    weight = 2.0 * rows / (tok_len + rows)
    current = (cotangent.astype(jnp.float32) * weight[:, None]).astype(jnp.bfloat16)
    xf = x_saved[0].astype(jnp.float32)
    centered_input = xf - jnp.mean(xf, -1, keepdims=True)
    variance = jnp.mean(centered_input * centered_input, -1, keepdims=True)
    inverse_deviation = lax.rsqrt(variance + 1e-05)
    standardized_input = centered_input * inverse_deviation
    gain_vector = gains[0]
    normalized_input = (standardized_input * gain_vector).astype(jnp.bfloat16)
    w_first, w_second = (
        lax.all_gather(w_in[0], "dp", axis=0, tiled=True),
        lax.all_gather(w_out[0], "dp", axis=1, tiled=True),
    )

    def project_all(normed_rows, grad_in):
        hidden = jnp.dot(normed_rows, w_first, preferred_element_type=jnp.float32)
        up_grad = jnp.dot(grad_in, w_second.T, preferred_element_type=jnp.float32)
        sig = jax.nn.sigmoid(hidden)
        hid_grad = (0.5 * up_grad * (sig + hidden * sig * (1.0 - sig))).astype(jnp.bfloat16)
        return jnp.dot(hid_grad, w_first.T, preferred_element_type=jnp.float32)

    def block_back():

        def run(grad_in):
            norm_gradient = project_all(normalized_input, grad_in)
            gain_partial = jnp.sum(norm_gradient * standardized_input, 0)
            gain_scaled = norm_gradient * gain_vector
            backward_result = inverse_deviation * (
                gain_scaled
                - jnp.mean(gain_scaled, -1, keepdims=True)
                - standardized_input * jnp.mean(gain_scaled * standardized_input, -1, keepdims=True)
            )
            return (
                (grad_in.astype(jnp.float32) + backward_result).astype(jnp.bfloat16),
                gain_partial,
            )

        return run

    def pass_through(grad_in):
        return (grad_in, jnp.zeros((width,), jnp.float32))

    segments = lax.axis_size("segment")
    my_segment = lax.axis_index("segment")
    gain_local = jnp.zeros((width,), jnp.float32)
    result = current
    for level in range(segments - 1, -1, -1):
        mine = my_segment == level
        updated, gain_partial = lax.cond(mine, block_back(), pass_through, current)
        result = jnp.where(mine, updated, result)
        gain_local = jnp.where(mine, gain_partial, gain_local)
        if level > 0:
            current = passed_along(updated, "segment", -1)
    gain_total = lax.psum(gain_local, "dp")
    return (result[None], gain_total[None])


def solution(mesh):
    in_specs = (
        P("segment", "dp", None),
        P("segment", None),
        P("segment", "dp", None),
        P("segment", None, "dp"),
        P("dp", None),
        P(),
    )
    out_specs = (P("segment", "dp", None), P("segment", None))
    return jax.shard_map(
        on_device, mesh=mesh, in_specs=in_specs, out_specs=out_specs, check_vma=False
    )
```

profile of v0, /device:TPU:8, one launch (start us, length us, event | category | flops | bytes accessed | tf_op | source)
XLA Modules:
  0.0 426.8 jit_solution(9842427514506412659)
XLA Ops:
  7.2 0.0 all-gather.7.cloned.1.call-start
  7.2 0.7 all-gather.7.cloned.1.call-update
  7.9 0.0 all-gather.5.cloned.1.call-start
  7.9 0.7 all-gather.5.cloned.1.call-update
  8.7 0.7 copy.17
  9.4 0.1 reduce-window.8
  9.5 0.1 reduce.5
  9.6 0.7 reduce.6
  10.3 0.1 convert_reduce_fusion.1
  10.4 0.7 select_reduce_fusion
  11.2 0.0 copy-start
  11.2 1.1 convert_reduce_fusion
  12.3 1.2 fusion.23
  13.6 0.0 copy-start.4
  13.6 1.5 fusion.21
  15.1 81.4 %all-gather.7.cloned.1.call-done = bf16[1,1536,3072]{2,1,0:T(8,128)(2,1)} async-done(((bf16[1,24,3072]{2,1,0:T(8,128)(2,1)}), bf16[1,1536,3072]{2,1,0:T(8,128)(2,1)}) %all-gather.7.cloned.1.call-update) | async-done | bytes 9437200 | tf_op jit(solution)/shard_map/all_gather | solution.py:34
  96.5 84.1 %all-gather.5.cloned.1.call-done = bf16[1,3072,1536]{1,2,0:T(8,128)(2,1)} async-done(((bf16[1,3072,24]{1,2,0:T(8,128)(2,1)}), bf16[1,3072,1536]{1,2,0:T(8,128)(2,1)}) %all-gather.5.cloned.1.call-update) | async-done | bytes 9437200 | tf_op jit(solution)/shard_map/all_gather | solution.py:35
  180.6 0.0 copy-done
  180.6 0.0 copy-done.4
  180.6 0.6 conditional.4
  180.7 0.6 broadcast.129
  181.3 1.3 collective-permute-start
  182.6 11.9 %collective-permute-done = bf16[128,1536]{1,0:T(8,128)(2,1)S(1)} collective-permute-done((bf16[128,1536]{1,0:T(8,128)(2,1)S(1)}, bf16[128,1536]{1,0:T(8,128)(2,1)S(1)}, u32[]{:S(2)}, u32[]{:S(2)}) %collective-permute-start) | collective-permute-done | bytes 393248 | tf_op jit(solution)/shard_map/ppermute | solution.py:10
  194.4 0.0 copy-start.2
  194.4 1.3 collective-permute-start.1
  195.7 11.0 %collective-permute-done.1 = bf16[128,1536]{1,0:T(8,128)(2,1)S(1)} collective-permute-done((bf16[128,1536]{1,0:T(8,128)(2,1)S(1)}, bf16[128,1536]{1,0:T(8,128)(2,1)S(1)}, u32[]{:S(2)}, u32[]{:S(2)}) %collective-permute-start.1) | collective-permute-done | bytes 393248 | tf_op jit(solution)/shard_map/ppermute | solution.py:10
  206.7 0.0 copy-done.2
  206.7 0.6 conditional.6
  206.7 0.6 broadcast.137
  207.3 1.3 collective-permute-start.2
  208.6 66.8 %collective-permute-done.2 = bf16[128,1536]{1,0:T(8,128)(2,1)S(1)} collective-permute-done((bf16[128,1536]{1,0:T(8,128)(2,1)S(1)}, bf16[128,1536]{1,0:T(8,128)(2,1)S(1)}, u32[]{:S(2)}, u32[]{:S(2)}) %collective-permute-start.2) | collective-permute-done | bytes 393248 | tf_op jit(solution)/shard_map/ppermute | solution.py:10
  275.4 0.0 copy-start.1
  275.4 0.0 copy-start.3
  275.4 20.4 %conditional.7 = (bf16[128,1536]{1,0:T(8,128)(2,1)S(1)}, f32[1536]{0:T(1024)S(1)}) conditional(s32[]{:T(128)} %convert_element_type.77, bf16[128,1536]{1,0:T(8,128)(2,1)S(1)} %collective-permute-done.2, (bf16[128,1536]{1,0:T(8,128)(2,1)S(1)}, f32[128,1]{0,1:T(1,128)}, bf16[3072,1536]{0,1:T(8,128)(2,1)}, bf16[128,1536]{1,0:T(8,128)(2,1)S(1)}, ...), branch_computations={%region_20.21_spmd, %region_21.25_spmd} | conditional | flops 3630562048 | bytes 36213296 | solution.py:72
  275.4 6.2 %fusion.28 = f32[128,3072]{1,0:T(8,128)} fusion(bf16[128,1536]{1,0:T(8,128)(2,1)S(1)} %get-tuple-element.84, bf16[1536,3072]{1,0:T(8,128)(2,1)} %get-tuple-element.85), kind=kOutput, calls=%fused_computation.69 | convolution fusion | flops 1207959552 | bytes 11403264 | tf_op jit(solution)/shard_map/cond/branch_1_fun/dot_general | solution.py:39
  281.7 0.0 copy-start.7
  281.7 12.7 %multiply_reduce_fusion.9 = (f32[1536]{0:T(1024)S(1)}, f32[128]{0:T(128)S(1)}, f32[128]{0:T(128)S(1)}, f32[128,1536]{1,0:T(8,128)}) fusion(f32[128,1536]{1,0:T(8,128)S(1)} %get-tuple-element.87, f32[1536]{0:T(1024)S(1)} %reduce.4, bf16[1536,3072]{1,0:T(8,128)(2,1)} %get-tuple-element.85, bf16[128,1536]{1,0:T(8,128)(2,1)S(1)} %get-tuple-element.81, ...), kind=kOutput, calls=%fused_computation.39 | convolution fusion | flops 2421029376 | bytes 22426624 | tf_op jit(solution)/shard_map/cond/branch_1_fun/dot_general | solution.py:43
  294.4 0.0 copy-done.7
  294.4 1.4 add_convert_fusion.3
  295.8 0.0 copy-done.1
  295.8 0.0 copy-done.3
  295.9 0.8 select_bitcast_fusion
  296.7 123.3 %psum.7 = f32[1,1536]{1,0:T(1,128)} all-reduce(f32[1,1536]{1,0:T(1,128)S(1)} %broadcast_in_dim.5), channel_id=1, replica_groups=mesh['segment'=4,'dp'=64] {'dp'}, use_global_device_ids=true, to_apply=%region_25.26 | all-reduce | flops 1536 | bytes 12288 | tf_op jit(solution)/shard_map/psum | solution.py:77
  (11 shorter events, 0.1 us)
Async XLA Ops:
  7.2 89.4 %all-gather.7.cloned.1.call-start = ((), (), s32[]{:S(2)}) async-start(), calls=%async_computation.1 | async-start | bytes 9584640 | tf_op jit(solution)/shard_map/all_gather | solution.py:34
  7.9 172.7 %all-gather.5.cloned.1.call-start = ((), (), s32[]{:S(2)}) async-start(), calls=%async_computation | async-start | bytes 9584640 | tf_op jit(solution)/shard_map/all_gather | solution.py:35
  11.2 169.4 %copy-start = (f32[1,1536]{1,0:T(1,128)S(1)}, f32[1,1536]{1,0:T(1,128)}, u32[]{:S(2)}) copy-start(f32[1,1536]{1,0:T(1,128)} %param.15) | copy-start | bytes 18436
  13.6 167.0 %copy-start.4 = (f32[128,1]{0,1:T(1,128)}, f32[128,1]{0,1:T(1,128)S(1)}, u32[]{:S(2)}) copy-start(f32[128,1]{0,1:T(1,128)S(1)} %get-tuple-element.189) | copy-start | bytes 1540
  181.3 13.2 %collective-permute-start = (bf16[128,1536]{1,0:T(8,128)(2,1)S(1)}, bf16[128,1536]{1,0:T(8,128)(2,1)S(1)}, u32[]{:S(2)}, u32[]{:S(2)}) collective-permute-start(bf16[128,1536]{1,0:T(8,128)(2,1)S(1)} %get-tuple-element.98), channel_id=1, source_target_pairs={{64,0},{128,64},{192,128},{65,1},{129,65},{193,129},{66,2},{130,66... | collective-permute-start | bytes 1179656 | tf_op jit(solution)/shard_map/ppermute | solution.py:10
  194.4 12.3 %copy-start.2 = (f32[1536]{0:T(1024)}, f32[1536]{0:T(1024)S(1)}, u32[]{:S(2)}) copy-start(f32[1536]{0:T(1024)S(1)} %get-tuple-element.104) | copy-start | bytes 18436
  194.4 12.3 %collective-permute-start.1 = (bf16[128,1536]{1,0:T(8,128)(2,1)S(1)}, bf16[128,1536]{1,0:T(8,128)(2,1)S(1)}, u32[]{:S(2)}, u32[]{:S(2)}) collective-permute-start(bf16[128,1536]{1,0:T(8,128)(2,1)S(1)} %get-tuple-element.99), channel_id=1, source_target_pairs={{64,0},{128,64},{192,128},{65,1},{129,65},{193,129},{66,2},{130,66... | collective-permute-start | bytes 1179656 | tf_op jit(solution)/shard_map/ppermute | solution.py:10
  207.3 68.1 %collective-permute-start.2 = (bf16[128,1536]{1,0:T(8,128)(2,1)S(1)}, bf16[128,1536]{1,0:T(8,128)(2,1)S(1)}, u32[]{:S(2)}, u32[]{:S(2)}) collective-permute-start(bf16[128,1536]{1,0:T(8,128)(2,1)S(1)} %get-tuple-element.100), channel_id=1, source_target_pairs={{64,0},{128,64},{192,128},{65,1},{129,65},{193,129},{66,2},{130,66... | collective-permute-start | bytes 1179656 | tf_op jit(solution)/shard_map/ppermute | solution.py:10
  275.4 20.4 %copy-start.1 = (f32[1536]{0:T(1024)S(1)}, f32[1536]{0:T(1024)}, u32[]{:S(2)}) copy-start(f32[1536]{0:T(1024)} %get-tuple-element.105) | copy-start | bytes 18436
  275.4 20.4 %copy-start.3 = (f32[1536]{0:T(1024)S(1)}, f32[1536]{0:T(1024)}, u32[]{:S(2)}) copy-start(f32[1536]{0:T(1024)} %copy-done.2) | copy-start | bytes 18436
  281.7 12.7 %copy-start.7 = (f32[128,1]{0,1:T(1,128)S(1)}, f32[128,1]{0,1:T(1,128)}, u32[]{:S(2)}) copy-start(f32[128,1]{0,1:T(1,128)} %get-tuple-element.82) | copy-start | bytes 1540 | tf_op jit(solution)/shard_map/cond
Sparse Core Ops, SparseCore 0:
  10.7 85.7 all-gather.6
  99.3 81.3 all-gather.4
where the time goes:
time: 433 us; the launch traced here: 427 us
  waiting for transfers between devices  257 us (59%)
  blocking collectives  123 us (28%)
  matrix products  18.9 us (4%)
  between operations  14.2 us (3%)
  other arithmetic  7.95 us (2%)
    psum x1, blocking collectives, on_device(): gain_total = lax.psum(gain_local, 'dp')  123 us
    ppermute x3, waiting for transfers between devices, passed_along(): return lax.ppermute(x, axis, pairs)  89.7 us
    all_gather x1, waiting for transfers between devices, on_device(): lax.all_gather(w_out[0], 'dp', axis=1, tiled=True)  84.1 us
    all_gather x1, waiting for transfers between devices, on_device(): lax.all_gather(w_in[0], 'dp', axis=0, tiled=True)  81.4 us
    dot_general x1, matrix products, project_all(): return jnp.dot(hid_grad, w_first.T, preferred_element_type=jnp.float32)  12.7 us
  transfers between devices with their start and end apart: 5, of which 5 were waited for; matrix products, arithmetic and copies ran while one was open for 1% of the time, Pallas kernels for 0%

commit v1 on v0

--- a/solution.py
+++ b/solution.py
@@ -1,7 +1,10 @@
 import jax
 import jax.numpy as jnp
 from jax import lax
-from jax.sharding import PartitionSpec as P
+import numpy as np
+from jax.sharding import Mesh, PartitionSpec as P
+
+DP = ("z", "y", "core")
 
 
 def passed_along(x, axis, by):
@@ -14,7 +17,7 @@
     rows = cotangent.shape[0]
     width = cotangent.shape[1]
     ends = jnp.cumsum(lengths)
-    position = lax.axis_index("dp") * rows + jnp.arange(rows, dtype=jnp.int32)
+    position = lax.axis_index(DP) * rows + jnp.arange(rows, dtype=jnp.int32)
     utter_hit = (position[:, None] >= ends[None, :]).astype(jnp.int32)
     utter = jnp.sum(utter_hit, 1)
     onehot = (utter[:, None] == jnp.arange(lengths.shape[0], dtype=jnp.int32)[None, :]).astype(
@@ -31,8 +34,8 @@
     gain_vector = gains[0]
     normalized_input = (standardized_input * gain_vector).astype(jnp.bfloat16)
     w_first, w_second = (
-        lax.all_gather(w_in[0], "dp", axis=0, tiled=True),
-        lax.all_gather(w_out[0], "dp", axis=1, tiled=True),
+        lax.all_gather(w_in[0], DP, axis=0, tiled=True),
+        lax.all_gather(w_out[0], DP, axis=1, tiled=True),
     )
 
     def project_all(normed_rows, grad_in):
@@ -74,20 +77,23 @@
         gain_local = jnp.where(mine, gain_partial, gain_local)
         if level > 0:
             current = passed_along(updated, "segment", -1)
-    gain_total = lax.psum(gain_local, "dp")
+    gain_total = lax.psum(lax.psum(lax.psum(gain_local, "core"), "y"), "z")
     return (result[None], gain_total[None])
 
 
 def solution(mesh):
+    n_seg, n_dp = mesh.devices.shape
+    sizes = dict(zip(("z", "y", "core"), (n_dp // 8, 4, 2)))
+    mesh = Mesh(np.asarray(mesh.devices).reshape(n_seg, sizes["z"], sizes["y"], sizes["core"]), ("segment",) + DP)
     in_specs = (
-        P("segment", "dp", None),
+        P("segment", DP, None),
         P("segment", None),
-        P("segment", "dp", None),
-        P("segment", None, "dp"),
-        P("dp", None),
+        P("segment", DP, None),
+        P("segment", None, DP),
+        P(DP, None),
         P(),
     )
-    out_specs = (P("segment", "dp", None), P("segment", None))
+    out_specs = (P("segment", DP, None), P("segment", None))
     return jax.shard_map(
         on_device, mesh=mesh, in_specs=in_specs, out_specs=out_specs, check_vma=False
     )

time: 433 us -> 333 us (0.77); the launches traced: 427 us -> 333 us
  blocking collectives: 123 us -> 29.2 us
    psum x1 -> x3, blocking collectives: 123 us -> 29.2 us  [on_device(): gain_total = lax.psum(lax.psum(lax.psum(gain_local, 'core'), 'y'), 'z')]
  transfers between devices with their start and end apart: 5 -> 5, of which waited for: 5 -> 5; matrix products, arithmetic and copies ran while one was open for 1% -> 2% of each run, Pallas kernels for 0% -> 0%
where the time goes in v1:
time: 333 us
  waiting for transfers between devices  257 us (77%)
  blocking collectives  29.2 us (9%)
  matrix products  18.9 us (6%)
  between operations  14.2 us (4%)
  other arithmetic  7.94 us (2%)
  starting transfers between devices  3.92 us (1%)
    ppermute x3, waiting for transfers between devices, passed_along(): return lax.ppermute(x, axis, pairs)  89.7 us
    all_gather x1, waiting for transfers between devices, on_device(): lax.all_gather(w_out[0], DP, axis=1, tiled=True)  84.1 us
    all_gather x1, waiting for transfers between devices, on_device(): lax.all_gather(w_in[0], DP, axis=0, tiled=True)  81.4 us
    psum x3, blocking collectives, on_device(): gain_total = lax.psum(lax.psum(lax.psum(gain_local, 'core'), 'y'), 'z')  29.2 us
    dot_general x1, matrix products, project_all(): return jnp.dot(hid_grad, w_first.T, preferred_element_type=jnp.float32)  12.7 us
  transfers between devices with their start and end apart: 5, of which 5 were waited for; matrix products, arithmetic and copies ran while one was open for 2% of the time, Pallas kernels for 0%

profile of v1, /device:TPU:8, one launch (start us, length us, event | category | flops | bytes accessed | tf_op | source)
XLA Modules:
  0.0 332.8 jit_solution(8786208565369843301)
XLA Ops:
  7.2 0.0 all-gather.7.cloned.1.call-start
  7.2 0.7 all-gather.7.cloned.1.call-update
  7.9 0.0 all-gather.5.cloned.1.call-start
  7.9 0.7 all-gather.5.cloned.1.call-update
  8.7 0.7 copy.17
  9.4 0.1 reduce-window.8
  9.5 0.1 reduce.5
  9.6 0.7 reduce.6
  10.4 0.1 convert_reduce_fusion.1
  10.4 0.7 select_reduce_fusion
  11.2 0.0 copy-start
  11.2 1.1 convert_reduce_fusion
  12.3 1.2 fusion.23
  13.6 0.0 copy-start.3
  13.6 1.5 fusion.21
  15.1 81.4 %all-gather.7.cloned.1.call-done = bf16[1,1536,3072]{2,1,0:T(8,128)(2,1)} async-done(((bf16[1,24,3072]{2,1,0:T(8,128)(2,1)}), bf16[1,1536,3072]{2,1,0:T(8,128)(2,1)}) %all-gather.7.cloned.1.call-update) | async-done | bytes 9437200 | tf_op jit(solution)/shard_map/all_gather | solution.py:37
  96.5 84.1 %all-gather.5.cloned.1.call-done = bf16[1,3072,1536]{1,2,0:T(8,128)(2,1)} async-done(((bf16[1,3072,24]{1,2,0:T(8,128)(2,1)}), bf16[1,3072,1536]{1,2,0:T(8,128)(2,1)}) %all-gather.5.cloned.1.call-update) | async-done | bytes 9437200 | tf_op jit(solution)/shard_map/all_gather | solution.py:38
  180.6 0.0 copy-done
  180.6 0.0 copy-done.3
  180.6 0.6 conditional.4
  180.7 0.6 broadcast.129
  181.2 1.3 collective-permute-start
  182.5 11.9 %collective-permute-done = bf16[128,1536]{1,0:T(8,128)(2,1)S(1)} collective-permute-done((bf16[128,1536]{1,0:T(8,128)(2,1)S(1)}, bf16[128,1536]{1,0:T(8,128)(2,1)S(1)}, u32[]{:S(2)}, u32[]{:S(2)}) %collective-permute-start) | collective-permute-done | bytes 393248 | tf_op jit(solution)/shard_map/ppermute | solution.py:13
  194.4 0.0 copy-start.1
  194.4 1.3 collective-permute-start.1
  195.7 11.0 %collective-permute-done.1 = bf16[128,1536]{1,0:T(8,128)(2,1)S(1)} collective-permute-done((bf16[128,1536]{1,0:T(8,128)(2,1)S(1)}, bf16[128,1536]{1,0:T(8,128)(2,1)S(1)}, u32[]{:S(2)}, u32[]{:S(2)}) %collective-permute-start.1) | collective-permute-done | bytes 393248 | tf_op jit(solution)/shard_map/ppermute | solution.py:13
  206.7 0.0 copy-done.1
  206.7 0.6 conditional.6
  206.7 0.6 broadcast.137
  207.3 1.3 collective-permute-start.2
  208.6 66.9 %collective-permute-done.2 = bf16[128,1536]{1,0:T(8,128)(2,1)S(1)} collective-permute-done((bf16[128,1536]{1,0:T(8,128)(2,1)S(1)}, bf16[128,1536]{1,0:T(8,128)(2,1)S(1)}, u32[]{:S(2)}, u32[]{:S(2)}) %collective-permute-start.2) | collective-permute-done | bytes 393248 | tf_op jit(solution)/shard_map/ppermute | solution.py:13
  275.4 20.4 %conditional.7 = (bf16[128,1536]{1,0:T(8,128)(2,1)S(1)}, f32[1536]{0:T(1024)S(1)}) conditional(s32[]{:T(128)} %convert_element_type.77, bf16[128,1536]{1,0:T(8,128)(2,1)S(1)} %collective-permute-done.2, (bf16[128,1536]{1,0:T(8,128)(2,1)S(1)}, f32[128,1]{0,1:T(1,128)}, bf16[3072,1536]{0,1:T(8,128)(2,1)}, bf16[128,1536]{1,0:T(8,128)(2,1)S(1)}, ...), branch_computations={%region_20.21_spmd, %region_21.25_spmd} | conditional | flops 3630562048 | bytes 36213296 | solution.py:75
  275.5 6.2 %fusion.28 = f32[128,3072]{1,0:T(8,128)} fusion(bf16[128,1536]{1,0:T(8,128)(2,1)S(1)} %get-tuple-element.84, bf16[1536,3072]{1,0:T(8,128)(2,1)} %get-tuple-element.85), kind=kOutput, calls=%fused_computation.69 | convolution fusion | flops 1207959552 | bytes 11403264 | tf_op jit(solution)/shard_map/cond/branch_1_fun/dot_general | solution.py:42
  281.7 0.0 copy-start.6
  281.7 12.7 %multiply_reduce_fusion.9 = (f32[1536]{0:T(1024)S(1)}, f32[128]{0:T(128)S(1)}, f32[128]{0:T(128)S(1)}, f32[128,1536]{1,0:T(8,128)}) fusion(f32[128,1536]{1,0:T(8,128)S(1)} %get-tuple-element.87, f32[1536]{0:T(1024)S(1)} %reduce.4, bf16[1536,3072]{1,0:T(8,128)(2,1)} %get-tuple-element.85, bf16[128,1536]{1,0:T(8,128)(2,1)S(1)} %get-tuple-element.81, ...), kind=kOutput, calls=%fused_computation.39 | convolution fusion | flops 2421029376 | bytes 22426624 | tf_op jit(solution)/shard_map/cond/branch_1_fun/dot_general | solution.py:46
  294.4 0.0 copy-done.6
  294.4 1.4 add_convert_fusion.3
  295.8 0.0 copy-start.2
  295.9 0.8 select_bitcast_fusion
  296.7 0.0 copy-done.2
  296.7 2.5 psum.21
  299.2 9.6 %psum.22 = f32[1536]{0:T(1024)S(1)} all-reduce(f32[1536]{0:T(1024)S(1)} %psum.21), channel_id=1, replica_groups=mesh['segment'=4,'z'=8,'y'=4,'core'=2] {'y'}, use_global_device_ids=true, to_apply=%region_26.27 | all-reduce | flops 1536 | bytes 12288 | tf_op jit(solution)/shard_map/psum | solution.py:80
  308.9 17.1 %psum.23 = f32[1,1536]{1,0:T(1,128)} all-reduce(f32[1,1536]{1,0:T(1,128)S(1)} %broadcast_in_dim.5), channel_id=1, replica_groups=mesh['segment'=4,'z'=8,'y'=4,'core'=2] {'z'}, use_global_device_ids=true, to_apply=%region_27.28 | all-reduce | flops 1536 | bytes 12288 | tf_op jit(solution)/shard_map/psum | solution.py:80
  (11 shorter events, 0.1 us)
Async XLA Ops:
  7.2 89.4 %all-gather.7.cloned.1.call-start = ((), (), s32[]{:S(2)}) async-start(), calls=%async_computation.1 | async-start | bytes 9584640 | tf_op jit(solution)/shard_map/all_gather | solution.py:37
  7.9 172.7 %all-gather.5.cloned.1.call-start = ((), (), s32[]{:S(2)}) async-start(), calls=%async_computation | async-start | bytes 9584640 | tf_op jit(solution)/shard_map/all_gather | solution.py:38
  11.2 169.4 %copy-start = (f32[1,1536]{1,0:T(1,128)S(1)}, f32[1,1536]{1,0:T(1,128)}, u32[]{:S(2)}) copy-start(f32[1,1536]{1,0:T(1,128)} %param.15) | copy-start | bytes 18436
  13.6 167.0 %copy-start.3 = (f32[128,1]{0,1:T(1,128)}, f32[128,1]{0,1:T(1,128)S(1)}, u32[]{:S(2)}) copy-start(f32[128,1]{0,1:T(1,128)S(1)} %get-tuple-element.189) | copy-start | bytes 1540
  181.2 13.2 %collective-permute-start = (bf16[128,1536]{1,0:T(8,128)(2,1)S(1)}, bf16[128,1536]{1,0:T(8,128)(2,1)S(1)}, u32[]{:S(2)}, u32[]{:S(2)}) collective-permute-start(bf16[128,1536]{1,0:T(8,128)(2,1)S(1)} %get-tuple-element.98), channel_id=1, source_target_pairs={{64,0},{128,64},{192,128},{65,1},{129,65},{193,129},{66,2},{130,66... | collective-permute-start | bytes 1179656 | tf_op jit(solution)/shard_map/ppermute | solution.py:13
  194.4 12.3 %copy-start.1 = (f32[1536]{0:T(1024)}, f32[1536]{0:T(1024)S(1)}, u32[]{:S(2)}) copy-start(f32[1536]{0:T(1024)S(1)} %get-tuple-element.104) | copy-start | bytes 18436
  194.4 12.3 %collective-permute-start.1 = (bf16[128,1536]{1,0:T(8,128)(2,1)S(1)}, bf16[128,1536]{1,0:T(8,128)(2,1)S(1)}, u32[]{:S(2)}, u32[]{:S(2)}) collective-permute-start(bf16[128,1536]{1,0:T(8,128)(2,1)S(1)} %get-tuple-element.99), channel_id=1, source_target_pairs={{64,0},{128,64},{192,128},{65,1},{129,65},{193,129},{66,2},{130,66... | collective-permute-start | bytes 1179656 | tf_op jit(solution)/shard_map/ppermute | solution.py:13
  207.3 68.2 %collective-permute-start.2 = (bf16[128,1536]{1,0:T(8,128)(2,1)S(1)}, bf16[128,1536]{1,0:T(8,128)(2,1)S(1)}, u32[]{:S(2)}, u32[]{:S(2)}) collective-permute-start(bf16[128,1536]{1,0:T(8,128)(2,1)S(1)} %get-tuple-element.100), channel_id=1, source_target_pairs={{64,0},{128,64},{192,128},{65,1},{129,65},{193,129},{66,2},{130,66... | collective-permute-start | bytes 1179656 | tf_op jit(solution)/shard_map/ppermute | solution.py:13
  281.7 12.7 %copy-start.6 = (f32[128,1]{0,1:T(1,128)S(1)}, f32[128,1]{0,1:T(1,128)}, u32[]{:S(2)}) copy-start(f32[128,1]{0,1:T(1,128)} %get-tuple-element.82) | copy-start | bytes 1540 | tf_op jit(solution)/shard_map/cond
  295.8 0.8 copy-start.2
Sparse Core Ops, SparseCore 0:
  10.7 85.7 all-gather.6
  99.3 81.3 all-gather.4

commit v2 on v1

v2 whole, which is shorter than its diff:
```python
import jax
import jax.numpy as jnp
import numpy as np
from jax import lax
from jax.experimental import pallas as pl
from jax.experimental.pallas import tpu as pltpu
from jax.sharding import Mesh, PartitionSpec as P

DP = ("z", "y", "core")
CHUNK = 512


def segment_kernel(z_ref, g_ref, xh_ref, inv_ref, gain_ref, w1_ref, w2_ref, out_ref, gp_ref, acc_ref):
    k = pl.program_id(0)

    @pl.when(k == 0)
    def _():
        acc_ref[...] = jnp.zeros_like(acc_ref)

    w1 = w1_ref[...]
    hidden = jnp.dot(z_ref[...], w1, preferred_element_type=jnp.float32)
    up_grad = jnp.dot(g_ref[...], w2_ref[...], preferred_element_type=jnp.float32)
    sig = jax.nn.sigmoid(hidden)
    hid_grad = (0.5 * up_grad * (sig + hidden * sig * (1.0 - sig))).astype(jnp.bfloat16)
    acc_ref[...] += lax.dot_general(
        hid_grad, w1, (((1,), (1,)), ((), ())), preferred_element_type=jnp.float32
    )

    @pl.when(k == pl.num_programs(0) - 1)
    def _():
        norm_gradient = acc_ref[...]
        standardized = xh_ref[...]
        gp_ref[...] = jnp.sum(norm_gradient * standardized, axis=0, keepdims=True)
        gain_scaled = norm_gradient * gain_ref[...]
        mean_e = jnp.mean(gain_scaled, axis=-1, keepdims=True)
        mean_ex = jnp.mean(gain_scaled * standardized, axis=-1, keepdims=True)
        back = inv_ref[...] * (gain_scaled - mean_e - standardized * mean_ex)
        out_ref[...] = (g_ref[...].astype(jnp.float32) + back).astype(out_ref.dtype)


def segment_back(normed, grad_in, standardized, inverse_deviation, gain_row, weights):
    rows, width = normed.shape
    steps = weights.shape[1] // 2 // CHUNK
    whole = lambda k: (0, 0)
    return pl.pallas_call(
        segment_kernel,
        grid=(steps,),
        in_specs=[
            pl.BlockSpec((rows, width), whole),
            pl.BlockSpec((rows, width), whole),
            pl.BlockSpec((rows, width), whole),
            pl.BlockSpec((rows, 1), whole),
            pl.BlockSpec((1, width), whole),
            pl.BlockSpec((width, CHUNK), lambda k: (0, k)),
            pl.BlockSpec((width, CHUNK), lambda k: (0, k + steps)),
        ],
        out_specs=[pl.BlockSpec((rows, width), whole), pl.BlockSpec((1, width), whole)],
        out_shape=[
            jax.ShapeDtypeStruct((rows, width), jnp.bfloat16),
            jax.ShapeDtypeStruct((1, width), jnp.float32),
        ],
        scratch_shapes=[pltpu.VMEM((rows, width), jnp.float32)],
        cost_estimate=pl.CostEstimate(
            flops=6 * rows * width * weights.shape[1] // 2,
            transcendentals=rows * weights.shape[1] // 2,
            bytes_accessed=2 * weights.size + 12 * rows * width,
        ),
    )(normed, grad_in, standardized, inverse_deviation, gain_row, weights, weights)


def on_device(x_saved, gains, w_in, w_out, cotangent, lengths):
    rows = cotangent.shape[0]
    width = cotangent.shape[1]
    ends = jnp.cumsum(lengths)
    position = lax.axis_index(DP) * rows + jnp.arange(rows, dtype=jnp.int32)
    utter_hit = (position[:, None] >= ends[None, :]).astype(jnp.int32)
    utter = jnp.sum(utter_hit, 1)
    onehot = (utter[:, None] == jnp.arange(lengths.shape[0], dtype=jnp.int32)[None, :]).astype(
        jnp.int32
    )
    tok_len = jnp.sum(onehot * lengths[None, :], 1).astype(jnp.float32)
    weight = 2.0 * rows / (tok_len + rows)
    current = (cotangent.astype(jnp.float32) * weight[:, None]).astype(jnp.bfloat16)
    xf = x_saved[0].astype(jnp.float32)
    centered_input = xf - jnp.mean(xf, -1, keepdims=True)
    variance = jnp.mean(centered_input * centered_input, -1, keepdims=True)
    inverse_deviation = lax.rsqrt(variance + 1e-05)
    standardized_input = centered_input * inverse_deviation
    gain_vector = gains[0]
    normalized_input = (standardized_input * gain_vector).astype(jnp.bfloat16)
    local = jnp.concatenate([w_in[0], w_out[0].T], axis=1)
    weights = lax.all_gather(local, DP, axis=0, tiled=True)

    def block_back(grad_in):
        return segment_back(
            normalized_input, grad_in, standardized_input, inverse_deviation,
            gain_vector[None, :], weights,
        )

    def pass_through(grad_in):
        return (grad_in, jnp.zeros((1, width), jnp.float32))

    segments = lax.axis_size("segment")
    my_segment = lax.axis_index("segment")
    result = current
    gain_local = jnp.zeros((1, width), jnp.float32)
    for level in range(segments - 1, -1, -1):
        mine = my_segment == level
        updated, gain_partial = lax.cond(mine, block_back, pass_through, current)
        result = jnp.where(mine, updated, result)
        gain_local = jnp.where(mine, gain_partial, gain_local)
        if level > 0:
            current = lax.ppermute(updated, "segment", [(level, level - 1)])
    gain_total = lax.psum(lax.psum(lax.psum(gain_local, "core"), "y"), "z")
    return (result[None], gain_total)


def solution(mesh):
    n_seg, n_dp = mesh.devices.shape
    shape = (n_seg, n_dp // 8, 4, 2)
    mesh = Mesh(np.asarray(mesh.devices).reshape(shape), ("segment",) + DP)
    in_specs = (
        P("segment", DP, None),
        P("segment", None),
        P("segment", DP, None),
        P("segment", None, DP),
        P(DP, None),
        P(),
    )
    out_specs = (P("segment", DP, None), P("segment", None))
    return jax.shard_map(
        on_device, mesh=mesh, in_specs=in_specs, out_specs=out_specs, check_vma=False
    )
```

time: 333 us -> 237 us (0.71)
  waiting for transfers between devices: 257 us -> 170 us
  matrix products: 18.9 us -> 0 us
  Pallas kernels: 0 us -> 11.2 us
    all_gather x2 -> x1, waiting for transfers between devices: 166 us -> 102 us  [on_device(): weights = lax.all_gather(local, DP, axis=0, tiled=True)]
    ppermute x3, waiting for transfers between devices: 89.7 us -> 67.4 us  [on_device(): current = lax.ppermute(updated, 'segment', [(level, level - 1)])]
    dot_general x2 -> x0, matrix products: 18.9 us -> none  [the longest x1 12.7 us: project_all(): return jnp.dot(hid_grad, w_first.T, preferred_element_type=jnp.float32)]
    pallas_call x0 -> x1, Pallas kernels: none -> 11.2 us  [segment_back(): pl.pallas_call(segment_kernel, grid=(steps,), in_specs=[pl.BlockSpec((row...]
  transfers between devices with their start and end apart: 5 -> 4, of which waited for: 5 -> 2; matrix products, arithmetic and copies ran while one was open for 2% -> 3% of each run, Pallas kernels for 0% -> 0%
where the time goes in v2:
time: 237 us
  waiting for transfers between devices  170 us (72%)
  blocking collectives  28.5 us (12%)
  between operations  14.2 us (6%)
  Pallas kernels  11.2 us (5%)
  other arithmetic  8.2 us (3%)
  starting transfers between devices  2.7 us (1%)
    all_gather x1, waiting for transfers between devices, on_device(): weights = lax.all_gather(local, DP, axis=0, tiled=True)  102 us
    ppermute x3, waiting for transfers between devices, on_device(): current = lax.ppermute(updated, 'segment', [(level, level - 1)])  67.4 us
    psum x3, blocking collectives, on_device(): gain_total = lax.psum(lax.psum(lax.psum(gain_local, 'core'), 'y'), 'z')  28.5 us
    pallas_call x1, Pallas kernels, segment_back(): pl.pallas_call(segment_kernel, grid=(steps,), in_specs=[pl.BlockSpec((row...  11.2 us
  transfers between devices with their start and end apart: 4, of which 2 were waited for; matrix products, arithmetic and copies ran while one was open for 3% of the time, Pallas kernels for 0%

profile of v2, /device:TPU:8, one launch (start us, length us, event | category | flops | bytes accessed | tf_op | source)
XLA Modules:
  0.0 236.8 jit_solution(15486900704668285749)
XLA Ops:
  7.2 0.0 all-gather.2.cloned.1.call-start
  7.2 1.7 pad_maximum_fusion
  8.9 0.0 all-gather.2.cloned.1.call-update
  9.0 0.7 copy.18
  9.7 0.1 reduce-window.8
  9.8 0.1 reduce.1
  9.9 0.7 reduce.2
  10.7 0.1 convert_reduce_fusion.1
  10.8 0.7 select_reduce_fusion
  11.5 1.1 convert_reduce_fusion
  12.6 1.2 fusion.3
  13.9 1.5 fusion.1
  15.4 102.1 %all-gather.2.cloned.1.call-done = bf16[1536,6144]{1,0:T(8,128)(2,1)} async-done(((bf16[24,6144]{1,0:T(8,128)(2,1)}), bf16[1536,6144]{1,0:T(8,128)(2,1)}) %all-gather.2.cloned.1.call-update) | async-done | bytes 18874384 | tf_op jit(solution)/shard_map/all_gather | solution.py:92
  117.6 0.7 collective-permute-start
  118.3 0.0 collective-permute-done
  118.3 0.1 conditional.5
  118.3 0.7 collective-permute-start.1
  119.0 0.0 collective-permute-done.1
  119.1 0.1 conditional.6
  119.1 1.3 collective-permute-start.2
  120.4 67.4 %collective-permute-done.2 = bf16[128,1536]{1,0:T(8,128)(2,1)S(1)} collective-permute-done((bf16[128,1536]{1,0:T(8,128)(2,1)S(1)}, bf16[128,1536]{1,0:T(8,128)(2,1)S(1)}, u32[]{:S(2)}, u32[]{:S(2)}) %collective-permute-start.2) | collective-permute-done | bytes 393248 | tf_op jit(solution)/shard_map/ppermute | solution.py:113
  187.8 12.7 %conditional.7 = ((bf16[128,1536]{1,0:T(8,128)(2,1)S(1)}, f32[1,1536]{1,0:T(1,128)S(1)})) conditional(s32[]{:T(128)} %convert_element_type.41, bf16[128,1536]{1,0:T(8,128)(2,1)S(1)} %collective-permute-done.2, (bf16[128,1536]{1,0:T(8,128)(2,1)S(1)}, bf16[128,1536]{1,0:T(8,128)(2,1)S(1)}, f32[128,1536]{1,0:T(8,128)S(1)}, f32[128,1]{0,1:T(1,128)S(1)}, ...), branch_computations={%region_11.12_spmd, %region_12.13_spmd} | conditional | flops 3623878656 | bytes 22021128 | solution.py:109
  187.8 0.7 copy.40.g_ref
  188.6 0.7 copy.22.inv_ref
  189.3 11.2 %branch_1_fun.7 = (bf16[128,1536]{1,0:T(8,128)(2,1)S(1)}, f32[1,1536]{1,0:T(1,128)S(1)}) custom-call(bf16[128,1536]{1,0:T(8,128)(2,1)S(1)} %get-tuple-element.70.z_ref, bf16[128,1536]{1,0:T(8,128)(2,1)} %copy.40.g_ref, f32[128,1536]{1,0:T(8,128)S(1)} %get-tuple-element.72.xh_ref, f32[128,1]{1,0:T(8,128)} %copy.22.inv_ref, ...), custom_call_target="tpu_custom_call" | custom-call | flops 3623878656 | bytes 21233664 | tf_op jit(solution)/shard_map/cond/branch_1_fun/pallas_call | solution.py:45
  200.6 0.8 select_bitcast_fusion
  201.4 2.5 %psum.21 = f32[1,1536]{1,0:T(1,128)S(1)} all-reduce(f32[1,1536]{1,0:T(1,128)S(1)} %broadcast_select_fusion.3), channel_id=1, replica_groups=mesh['segment'=4,'z'=8,'y'=4,'core'=2] {'core'}, use_global_device_ids=true, to_apply=%region_13.14 | all-reduce | flops 1536 | bytes 12288 | tf_op jit(solution)/shard_map/psum | solution.py:114
  203.9 9.7 %psum.22 = f32[1,1536]{1,0:T(1,128)S(1)} all-reduce(f32[1,1536]{1,0:T(1,128)S(1)} %psum.21), channel_id=1, replica_groups=mesh['segment'=4,'z'=8,'y'=4,'core'=2] {'y'}, use_global_device_ids=true, to_apply=%region_14.15 | all-reduce | flops 1536 | bytes 12288 | tf_op jit(solution)/shard_map/psum | solution.py:114
  213.6 16.3 %psum.23 = f32[1,1536]{1,0:T(1,128)} all-reduce(f32[1,1536]{1,0:T(1,128)S(1)} %psum.22), channel_id=1, replica_groups=mesh['segment'=4,'z'=8,'y'=4,'core'=2] {'z'}, use_global_device_ids=true, to_apply=%region_15.16 | all-reduce | flops 1536 | bytes 12288 | tf_op jit(solution)/shard_map/psum | solution.py:114
  (12 shorter events, 0.2 us)
Async XLA Ops:
  7.2 110.3 %all-gather.2.cloned.1.call-start = ((), (), s32[]{:S(2)}) async-start(), calls=%async_computation | async-start | bytes 19169280 | tf_op jit(solution)/shard_map/all_gather | solution.py:92
  117.6 0.7 collective-permute-start
  118.3 0.7 collective-permute-start.1
  119.1 68.7 %collective-permute-start.2 = (bf16[128,1536]{1,0:T(8,128)(2,1)S(1)}, bf16[128,1536]{1,0:T(8,128)(2,1)S(1)}, u32[]{:S(2)}, u32[]{:S(2)}) collective-permute-start(bf16[128,1536]{1,0:T(8,128)(2,1)S(1)} %get-tuple-element.88), channel_id=1, source_target_pairs={{64,0},{65,1},{66,2},{67,3},{68,4},{69,5},{70,6},{71,7},{72,8},{73... | collective-permute-start | bytes 1179656 | tf_op jit(solution)/shard_map/ppermute | solution.py:113
Sparse Core Ops, SparseCore 0:
  11.3 106.1 all-gather.1

commit v3 on v2

--- a/solution.py
+++ b/solution.py
@@ -7,23 +7,45 @@
 from jax.sharding import Mesh, PartitionSpec as P
 
 DP = ("z", "y", "core")
-CHUNK = 512
+CHUNK = 768
 
 
-def segment_kernel(z_ref, g_ref, xh_ref, inv_ref, gain_ref, w1_ref, w2_ref, out_ref, gp_ref, acc_ref):
+def act_kernel(z_ref, w1_ref, act_ref):
+    hidden = jnp.dot(z_ref[...], w1_ref[...], preferred_element_type=jnp.float32)
+    sig = jax.nn.sigmoid(hidden)
+    act_ref[...] = sig + hidden * sig * (1.0 - sig)
+
+
+def hidden_slope(normed, weights):
+    rows, width = normed.shape
+    ff = weights.shape[1] // 2
+    return pl.pallas_call(
+        act_kernel,
+        grid=(ff // CHUNK,),
+        in_specs=[
+            pl.BlockSpec((rows, width), lambda k: (0, 0)),
+            pl.BlockSpec((width, CHUNK), lambda k: (0, k)),
+        ],
+        out_specs=pl.BlockSpec((rows, CHUNK), lambda k: (0, k)),
+        out_shape=jax.ShapeDtypeStruct((rows, ff), jnp.float32),
+        cost_estimate=pl.CostEstimate(
+            flops=2 * rows * width * ff, transcendentals=rows * ff,
+            bytes_accessed=2 * width * ff + 4 * rows * ff + 2 * rows * width,
+        ),
+    )(normed, weights)
+
+
+def segment_kernel(g_ref, act_ref, xh_ref, inv_ref, gain_ref, w1_ref, w2_ref, out_ref, gp_ref, acc_ref):
     k = pl.program_id(0)
 
     @pl.when(k == 0)
     def _():
         acc_ref[...] = jnp.zeros_like(acc_ref)
 
-    w1 = w1_ref[...]
-    hidden = jnp.dot(z_ref[...], w1, preferred_element_type=jnp.float32)
     up_grad = jnp.dot(g_ref[...], w2_ref[...], preferred_element_type=jnp.float32)
-    sig = jax.nn.sigmoid(hidden)
-    hid_grad = (0.5 * up_grad * (sig + hidden * sig * (1.0 - sig))).astype(jnp.bfloat16)
+    hid_grad = (0.5 * up_grad * act_ref[...]).astype(jnp.bfloat16)
     acc_ref[...] += lax.dot_general(
-        hid_grad, w1, (((1,), (1,)), ((), ())), preferred_element_type=jnp.float32
+        hid_grad, w1_ref[...], (((1,), (1,)), ((), ())), preferred_element_type=jnp.float32
     )
 
     @pl.when(k == pl.num_programs(0) - 1)
@@ -38,8 +60,8 @@
         out_ref[...] = (g_ref[...].astype(jnp.float32) + back).astype(out_ref.dtype)
 
 
-def segment_back(normed, grad_in, standardized, inverse_deviation, gain_row, weights):
-    rows, width = normed.shape
+def segment_back(grad_in, slope, standardized, inverse_deviation, gain_row, weights):
+    rows, width = grad_in.shape
     steps = weights.shape[1] // 2 // CHUNK
     whole = lambda k: (0, 0)
     return pl.pallas_call(
@@ -47,7 +69,7 @@
         grid=(steps,),
         in_specs=[
             pl.BlockSpec((rows, width), whole),
-            pl.BlockSpec((rows, width), whole),
+            pl.BlockSpec((rows, CHUNK), lambda k: (0, k)),
             pl.BlockSpec((rows, width), whole),
             pl.BlockSpec((rows, 1), whole),
             pl.BlockSpec((1, width), whole),
@@ -61,11 +83,11 @@
         ],
         scratch_shapes=[pltpu.VMEM((rows, width), jnp.float32)],
         cost_estimate=pl.CostEstimate(
-            flops=6 * rows * width * weights.shape[1] // 2,
-            transcendentals=rows * weights.shape[1] // 2,
-            bytes_accessed=2 * weights.size + 12 * rows * width,
+            flops=4 * rows * width * weights.shape[1] // 2,
+            transcendentals=0,
+            bytes_accessed=2 * weights.size + 2 * rows * weights.shape[1] + 12 * rows * width,
         ),
-    )(normed, grad_in, standardized, inverse_deviation, gain_row, weights, weights)
+    )(grad_in, slope, standardized, inverse_deviation, gain_row, weights, weights)
 
 
 def on_device(x_saved, gains, w_in, w_out, cotangent, lengths):
@@ -91,10 +113,11 @@
     local = jnp.concatenate([w_in[0], w_out[0].T], axis=1)
     weights = lax.all_gather(local, DP, axis=0, tiled=True)
 
+    slope = hidden_slope(normalized_input, weights)
+
     def block_back(grad_in):
         return segment_back(
-            normalized_input, grad_in, standardized_input, inverse_deviation,
-            gain_vector[None, :], weights,
+            grad_in, slope, standardized_input, inverse_deviation, gain_vector[None, :], weights
         )
 
     def pass_through(grad_in):

time: 237 us -> 240 us (1.013)
  waiting for transfers between devices: 170 us -> 163 us
  Pallas kernels: 11.2 us -> 15.4 us
  local copies, waits for them, and re-layouts: 2.32 us -> 5.54 us
    pallas_call x0 -> x1, Pallas kernels: none -> 5.44 us  [hidden_slope(): pl.pallas_call(act_kernel, grid=(ff // CHUNK,), in_specs=[pl.BlockSpec((r...]
    ppermute x3, waiting for transfers between devices: 67.4 us -> 63.1 us  [on_device(): current = lax.ppermute(updated, 'segment', [(level, level - 1)])]
where the time goes in v3:
time: 240 us
  waiting for transfers between devices  163 us (68%)
  blocking collectives  28.4 us (12%)
  Pallas kernels  15.4 us (6%)
  between operations  14.2 us (6%)
  other arithmetic  10.1 us (4%)
  local copies, waits for them, and re-layouts  5.54 us (2%)
  starting transfers between devices  2.68 us (1%)
    all_gather x1, waiting for transfers between devices, on_device(): weights = lax.all_gather(local, DP, axis=0, tiled=True)  100 us
    ppermute x3, waiting for transfers between devices, on_device(): current = lax.ppermute(updated, 'segment', [(level, level - 1)])  63.1 us
    psum x3, blocking collectives, on_device(): gain_total = lax.psum(lax.psum(lax.psum(gain_local, 'core'), 'y'), 'z')  28.4 us
    pallas_call x1, Pallas kernels, segment_back(): pl.pallas_call(segment_kernel, grid=(steps,), in_specs=[pl.BlockSpec((row...  9.95 us
    pallas_call x1, Pallas kernels, hidden_slope(): pl.pallas_call(act_kernel, grid=(ff // CHUNK,), in_specs=[pl.BlockSpec((r...  5.44 us
  transfers between devices with their start and end apart: 4, of which 2 were waited for; matrix products, arithmetic and copies ran while one was open for 3% of the time, Pallas kernels for 0%

profile of v3, /device:TPU:8, one launch (start us, length us, event | category | flops | bytes accessed | tf_op | source)
XLA Modules:
  0.0 239.8 jit_solution(11603230078333646603)
XLA Ops:
  7.2 0.0 copy-start
  7.2 0.0 all-gather.2.cloned.1.call-start
  7.2 1.7 pad_maximum_fusion
  9.0 0.0 all-gather.2.cloned.1.call-update
  9.0 0.7 copy.18
  9.7 0.1 reduce-window.8
  9.8 0.1 reduce.1
  10.0 0.7 reduce.2
  10.7 0.1 convert_reduce_fusion.1
  10.8 0.7 select_reduce_fusion
  11.5 1.1 convert_reduce_fusion
  12.7 1.2 fusion.3
  13.9 0.5 fusion.4
  14.5 2.2 fusion.1
  16.6 100.3 %all-gather.2.cloned.1.call-done.w1_ref = bf16[1536,6144]{1,0:T(8,128)(2,1)} async-done(((bf16[24,6144]{1,0:T(8,128)(2,1)}), bf16[1536,6144]{1,0:T(8,128)(2,1)}) %all-gather.2.cloned.1.call-update) | async-done | bytes 18874384 | tf_op jit(solution)/shard_map/all_gather | solution.py:114
  116.9 5.4 %shard_map.77 = f32[128,3072]{1,0:T(8,128)S(1)} custom-call(bf16[128,1536]{1,0:T(8,128)(2,1)} %get-tuple-element.167.z_ref, bf16[1536,6144]{1,0:T(8,128)(2,1)} %all-gather.2.cloned.1.call-done.w1_ref), custom_call_target="tpu_custom_call" | custom-call | flops 1207959552 | bytes 11403264 | tf_op jit(solution)/shard_map/pallas_call | solution.py:22
  122.4 0.0 copy-done
  122.4 0.1 conditional.4
  122.5 0.7 collective-permute-start
  123.2 0.0 collective-permute-done
  123.2 1.4 conditional.5
  123.2 0.7 copy.27
  123.9 0.6 broadcast.58
  124.5 0.7 collective-permute-start.1
  125.2 0.0 collective-permute-done.1
  125.2 1.4 conditional.6
  125.3 0.8 copy.31
  126.0 0.6 broadcast.59
  126.6 1.3 collective-permute-start.2
  127.9 63.1 %collective-permute-done.2 = bf16[128,1536]{1,0:T(8,128)(2,1)S(1)} collective-permute-done((bf16[128,1536]{1,0:T(8,128)(2,1)}, bf16[128,1536]{1,0:T(8,128)(2,1)S(1)}, u32[]{:S(2)}, u32[]{:S(2)}) %collective-permute-start.2) | collective-permute-done | bytes 393248 | tf_op jit(solution)/shard_map/ppermute | solution.py:136
  191.0 12.0 %conditional.7 = ((bf16[128,1536]{1,0:T(8,128)(2,1)S(1)}, f32[1,1536]{1,0:T(1,128)})) conditional(s32[]{:T(128)} %convert_element_type.41, bf16[128,1536]{1,0:T(8,128)(2,1)S(1)} %collective-permute-done.2, (bf16[128,1536]{1,0:T(8,128)(2,1)S(1)}, f32[128,3072]{1,0:T(8,128)S(1)}, f32[128,1536]{1,0:T(8,128)S(1)}, f32[128,1]{0,1:T(1,128)}, ...), branch_computations={%region_11.12_spmd, %region_12.13_spmd} | conditional | flops 2415919104 | bytes 23593992 | solution.py:132
  191.0 0.8 copy.40.g_ref
  191.7 1.3 copy.22.inv_ref
  193.0 10.0 %branch_1_fun.7 = (bf16[128,1536]{1,0:T(8,128)(2,1)S(1)}, f32[1,1536]{1,0:T(1,128)}) custom-call(bf16[128,1536]{1,0:T(8,128)(2,1)} %copy.40.g_ref, f32[128,3072]{1,0:T(8,128)S(1)} %get-tuple-element.71.act_ref, f32[128,1536]{1,0:T(8,128)S(1)} %get-tuple-element.72.xh_ref, f32[128,1]{1,0:T(8,128)} %copy.22.inv_ref, f32[1,1536]{1,0:T(1,128)S(1)} %get-tuple-element.74.gain_ref, ...), custom_call_target="tpu_custom_call" | custom-call | flops 2415919104 | bytes 22806528 | tf_op jit(solution)/shard_map/cond/branch_1_fun/pallas_call | solution.py:67
  203.0 0.8 select_bitcast_fusion
  203.8 0.7 broadcast_select_fusion.3
  204.5 2.5 %psum.21 = f32[1,1536]{1,0:T(1,128)S(1)} all-reduce(f32[1,1536]{1,0:T(1,128)S(1)} %broadcast_select_fusion.3), channel_id=1, replica_groups=mesh['segment'=4,'z'=8,'y'=4,'core'=2] {'core'}, use_global_device_ids=true, to_apply=%region_13.14 | all-reduce | flops 1536 | bytes 12288 | tf_op jit(solution)/shard_map/psum | solution.py:137
  207.0 9.6 %psum.22 = f32[1,1536]{1,0:T(1,128)S(1)} all-reduce(f32[1,1536]{1,0:T(1,128)S(1)} %psum.21), channel_id=1, replica_groups=mesh['segment'=4,'z'=8,'y'=4,'core'=2] {'y'}, use_global_device_ids=true, to_apply=%region_14.15 | all-reduce | flops 1536 | bytes 12288 | tf_op jit(solution)/shard_map/psum | solution.py:137
  216.6 16.3 %psum.23 = f32[1,1536]{1,0:T(1,128)} all-reduce(f32[1,1536]{1,0:T(1,128)S(1)} %psum.22), channel_id=1, replica_groups=mesh['segment'=4,'z'=8,'y'=4,'core'=2] {'z'}, use_global_device_ids=true, to_apply=%region_15.16 | all-reduce | flops 1536 | bytes 12288 | tf_op jit(solution)/shard_map/psum | solution.py:137
  (5 shorter events, 0.1 us)
Async XLA Ops:
  7.2 115.2 %copy-start = (f32[1,1536]{1,0:T(1,128)S(1)}, f32[1,1536]{1,0:T(1,128)}, u32[]{:S(2)}) copy-start(f32[1,1536]{1,0:T(1,128)} %param.15) | copy-start | bytes 18436
  7.2 109.8 %all-gather.2.cloned.1.call-start = ((), (), s32[]{:S(2)}) async-start(), calls=%async_computation | async-start | bytes 19169280 | tf_op jit(solution)/shard_map/all_gather | solution.py:114
  122.5 0.7 collective-permute-start
  124.5 0.7 collective-permute-start.1
  126.6 64.4 %collective-permute-start.2 = (bf16[128,1536]{1,0:T(8,128)(2,1)}, bf16[128,1536]{1,0:T(8,128)(2,1)S(1)}, u32[]{:S(2)}, u32[]{:S(2)}) collective-permute-start(bf16[128,1536]{1,0:T(8,128)(2,1)} %get-tuple-element.88), channel_id=1, source_target_pairs={{64,0},{65,1},{66,2},{67,3},{68,4},{69,5},{70,6},{71,7},{72,8},{73... | collective-permute-start | bytes 1179656 | tf_op jit(solution)/shard_map/ppermute | solution.py:136
Sparse Core Ops, SparseCore 0:
  10.7 106.1 all-gather.1

commit v4 on v3

--- a/solution.py
+++ b/solution.py
@@ -35,6 +35,68 @@
     )(normed, weights)
 
 
+def fused_kernel(z_ref, g_ref, xh_ref, inv_ref, gain_ref, w1_ref, w2_ref, out_ref, gp_ref, acc_ref):
+    k = pl.program_id(0)
+
+    @pl.when(k == 0)
+    def _():
+        acc_ref[...] = jnp.zeros_like(acc_ref)
+
+    w1 = w1_ref[...]
+    hidden = jnp.dot(z_ref[...], w1, preferred_element_type=jnp.float32)
+    up_grad = jnp.dot(g_ref[...], w2_ref[...], preferred_element_type=jnp.float32)
+    sig = jax.nn.sigmoid(hidden)
+    hid_grad = (0.5 * up_grad * (sig + hidden * sig * (1.0 - sig))).astype(jnp.bfloat16)
+    acc_ref[...] += lax.dot_general(
+        hid_grad, w1, (((1,), (1,)), ((), ())), preferred_element_type=jnp.float32
+    )
+
+    @pl.when(k == pl.num_programs(0) - 1)
+    def _():
+        norm_backward(acc_ref, xh_ref, inv_ref, gain_ref, g_ref, out_ref, gp_ref)
+
+
+def norm_backward(acc_ref, xh_ref, inv_ref, gain_ref, g_ref, out_ref, gp_ref):
+    norm_gradient = acc_ref[...]
+    standardized = xh_ref[...]
+    gp_ref[...] = jnp.sum(norm_gradient * standardized, axis=0, keepdims=True)
+    gain_scaled = norm_gradient * gain_ref[...]
+    mean_e = jnp.mean(gain_scaled, axis=-1, keepdims=True)
+    mean_ex = jnp.mean(gain_scaled * standardized, axis=-1, keepdims=True)
+    back = inv_ref[:, 0:1] * (gain_scaled - mean_e - standardized * mean_ex)
+    out_ref[...] = (g_ref[...].astype(jnp.float32) + back).astype(out_ref.dtype)
+
+
+def fused_back(normed, grad_in, standardized, inverse_deviation, gain_row, weights):
+    rows, width = normed.shape
+    steps = weights.shape[1] // 2 // CHUNK
+    whole = lambda k: (0, 0)
+    return pl.pallas_call(
+        fused_kernel,
+        grid=(steps,),
+        in_specs=[
+            pl.BlockSpec((rows, width), whole),
+            pl.BlockSpec((rows, width), whole),
+            pl.BlockSpec((rows, width), whole),
+            pl.BlockSpec(inverse_deviation.shape, whole),
+            pl.BlockSpec((1, width), whole),
+            pl.BlockSpec((width, CHUNK), lambda k: (0, k)),
+            pl.BlockSpec((width, CHUNK), lambda k: (0, k + steps)),
+        ],
+        out_specs=[pl.BlockSpec((rows, width), whole), pl.BlockSpec((1, width), whole)],
+        out_shape=[
+            jax.ShapeDtypeStruct((rows, width), jnp.bfloat16),
+            jax.ShapeDtypeStruct((1, width), jnp.float32),
+        ],
+        scratch_shapes=[pltpu.VMEM((rows, width), jnp.float32)],
+        cost_estimate=pl.CostEstimate(
+            flops=6 * rows * width * weights.shape[1] // 2,
+            transcendentals=rows * weights.shape[1] // 2,
+            bytes_accessed=2 * weights.size + 12 * rows * width,
+        ),
+    )(normed, grad_in, standardized, inverse_deviation, gain_row, weights, weights)
+
+
 def segment_kernel(g_ref, act_ref, xh_ref, inv_ref, gain_ref, w1_ref, w2_ref, out_ref, gp_ref, acc_ref):
     k = pl.program_id(0)
 
@@ -50,14 +112,7 @@
 
     @pl.when(k == pl.num_programs(0) - 1)
     def _():
-        norm_gradient = acc_ref[...]
-        standardized = xh_ref[...]
-        gp_ref[...] = jnp.sum(norm_gradient * standardized, axis=0, keepdims=True)
-        gain_scaled = norm_gradient * gain_ref[...]
-        mean_e = jnp.mean(gain_scaled, axis=-1, keepdims=True)
-        mean_ex = jnp.mean(gain_scaled * standardized, axis=-1, keepdims=True)
-        back = inv_ref[...] * (gain_scaled - mean_e - standardized * mean_ex)
-        out_ref[...] = (g_ref[...].astype(jnp.float32) + back).astype(out_ref.dtype)
+        norm_backward(acc_ref, xh_ref, inv_ref, gain_ref, g_ref, out_ref, gp_ref)
 
 
 def segment_back(grad_in, slope, standardized, inverse_deviation, gain_row, weights):
@@ -71,7 +126,7 @@
             pl.BlockSpec((rows, width), whole),
             pl.BlockSpec((rows, CHUNK), lambda k: (0, k)),
             pl.BlockSpec((rows, width), whole),
-            pl.BlockSpec((rows, 1), whole),
+            pl.BlockSpec(inverse_deviation.shape, whole),
             pl.BlockSpec((1, width), whole),
             pl.BlockSpec((width, CHUNK), lambda k: (0, k)),
             pl.BlockSpec((width, CHUNK), lambda k: (0, k + steps)),
@@ -113,27 +168,38 @@
     local = jnp.concatenate([w_in[0], w_out[0].T], axis=1)
     weights = lax.all_gather(local, DP, axis=0, tiled=True)
 
-    slope = hidden_slope(normalized_input, weights)
-
-    def block_back(grad_in):
-        return segment_back(
-            grad_in, slope, standardized_input, inverse_deviation, gain_vector[None, :], weights
-        )
-
-    def pass_through(grad_in):
-        return (grad_in, jnp.zeros((1, width), jnp.float32))
-
+    inverse_rows = jnp.broadcast_to(inverse_deviation, (rows, 128))
+    gain_row = gain_vector[None, :]
     segments = lax.axis_size("segment")
     my_segment = lax.axis_index("segment")
+    first = segments - 1
+    slope = lax.cond(
+        my_segment == first,
+        lambda: jnp.zeros((rows, weights.shape[1] // 2), jnp.float32),
+        lambda: hidden_slope(normalized_input, weights),
+    )
+
+    def keep(grad_in, kept, kept_gain):
+        return kept, kept_gain
+
     result = current
     gain_local = jnp.zeros((1, width), jnp.float32)
-    for level in range(segments - 1, -1, -1):
-        mine = my_segment == level
-        updated, gain_partial = lax.cond(mine, block_back, pass_through, current)
-        result = jnp.where(mine, updated, result)
-        gain_local = jnp.where(mine, gain_partial, gain_local)
+    for level in range(first, -1, -1):
+        if level == first:
+            def mine(grad_in, kept, kept_gain):
+                return fused_back(
+                    normalized_input, grad_in, standardized_input, inverse_rows, gain_row, weights
+                )
+        else:
+            def mine(grad_in, kept, kept_gain):
+                return segment_back(
+                    grad_in, slope, standardized_input, inverse_rows, gain_row, weights
+                )
+        result, gain_local = lax.cond(
+            my_segment == level, mine, keep, current, result, gain_local
+        )
         if level > 0:
-            current = lax.ppermute(updated, "segment", [(level, level - 1)])
+            current = lax.ppermute(result, "segment", [(level, level - 1)])
     gain_total = lax.psum(lax.psum(lax.psum(gain_local, "core"), "y"), "z")
     return (result[None], gain_total)
 

time: 240 us -> 230 us (0.958)
  other arithmetic: 10.1 us -> 5.3 us
  local copies, waits for them, and re-layouts: 5.54 us -> 1.59 us
    ppermute x3, waiting for transfers between devices: 63.1 us -> 57.5 us  [on_device(): current = lax.ppermute(result, 'segment', [(level, level - 1)])]
    all_gather x1, waiting for transfers between devices: 100 us -> 104 us  [on_device(): weights = lax.all_gather(local, DP, axis=0, tiled=True)]
    another operation x5 -> x1, local copies, waits for them, and re-layouts: 3.26 us -> 0.75 us
  transfers between devices with their start and end apart: 4 -> 4, of which waited for: 2 -> 2; matrix products, arithmetic and copies ran while one was open for 3% -> 2% of each run, Pallas kernels for 0% -> 2%
where the time goes in v4:
time: 230 us; the launch traced here: 229 us
  waiting for transfers between devices  162 us (70%)
  blocking collectives  28.4 us (12%)
  Pallas kernels  15.3 us (7%)
  between operations  14.2 us (6%)
  other arithmetic  5.3 us (2%)
  starting transfers between devices  2.69 us (1%)
    all_gather x1, waiting for transfers between devices, on_device(): weights = lax.all_gather(local, DP, axis=0, tiled=True)  104 us
    ppermute x3, waiting for transfers between devices, on_device(): current = lax.ppermute(result, 'segment', [(level, level - 1)])  57.5 us
    psum x3, blocking collectives, on_device(): gain_total = lax.psum(lax.psum(lax.psum(gain_local, 'core'), 'y'), 'z')  28.4 us
    pallas_call x1, Pallas kernels, segment_back(): pl.pallas_call(segment_kernel, grid=(steps,), in_specs=[pl.BlockSpec((row...  10 us
    pallas_call x1, Pallas kernels, hidden_slope(): pl.pallas_call(act_kernel, grid=(ff // CHUNK,), in_specs=[pl.BlockSpec((r...  5.32 us
  transfers between devices with their start and end apart: 4, of which 2 were waited for; matrix products, arithmetic and copies ran while one was open for 2% of the time, Pallas kernels for 2%

profile of v4, /device:TPU:8, one launch (start us, length us, event | category | flops | bytes accessed | tf_op | source)
XLA Modules:
  0.0 229.2 jit_solution(8295566884453518070)
XLA Ops:
  7.2 0.0 copy-start
  7.2 0.0 copy-start.1
  7.2 0.0 all-gather.2.cloned.1.call-start
  7.2 1.8 pad_maximum_fusion
  9.0 0.0 all-gather.2.cloned.1.call-update
  9.0 0.7 copy.10
  9.8 0.1 reduce-window.8
  9.9 0.1 reduce.1
  10.0 0.7 reduce.2
  10.7 0.1 convert_reduce_fusion.1
  10.8 0.7 select_reduce_fusion
  11.6 0.0 copy-start.2
  11.6 1.1 convert_reduce_fusion
  12.7 0.0 copy-done
  12.7 0.3 fusion.3
  13.0 0.0 copy-done.1
  13.0 0.3 fusion.1
  13.4 104.1 %all-gather.2.cloned.1.call-done = bf16[1536,6144]{1,0:T(8,128)(2,1)} async-done(((bf16[24,6144]{1,0:T(8,128)(2,1)}), bf16[1536,6144]{1,0:T(8,128)(2,1)}) %all-gather.2.cloned.1.call-update) | async-done | bytes 18874384 | tf_op jit(solution)/shard_map/all_gather | solution.py:169
  117.5 0.1 broadcast_in_dim.9
  117.6 0.0 copy-done.2
  117.6 0.8 conditional.5
  117.6 0.7 copy.11
  118.4 0.7 collective-permute-start
  119.1 5.3 %conditional.6 = (f32[128,3072]{1,0:T(8,128)S(1)}) conditional(s32[]{:T(128)} %convert_element_type.45, (bf16[128,1536]{1,0:T(8,128)(2,1)S(1)}, bf16[1536,6144]{1,0:T(8,128)(2,1)}) %tuple.44, () %tuple.45), branch_computations={%region_7.8_spmd, %region_8.9_spmd} | conditional | flops 1207959552 | bytes 11403272 | solution.py:176
  119.1 5.3 %branch_0_fun.1 = f32[128,3072]{1,0:T(8,128)S(1)} custom-call(bf16[128,1536]{1,0:T(8,128)(2,1)S(1)} %get-tuple-element.81.z_ref, bf16[1536,6144]{1,0:T(8,128)(2,1)} %get-tuple-element.82.w1_ref), custom_call_target="tpu_custom_call" | custom-call | flops 1207959552 | bytes 11403264 | tf_op jit(solution)/shard_map/cond/branch_0_fun/pallas_call | solution.py:22
  124.4 0.0 collective-permute-done
  124.4 0.7 collective-permute-start.1
  125.1 0.0 collective-permute-done.1
  125.2 1.3 collective-permute-start.2
  126.5 57.4 %collective-permute-done.2 = bf16[128,1536]{1,0:T(8,128)(2,1)S(1)} collective-permute-done((bf16[128,1536]{1,0:T(8,128)(2,1)}, bf16[128,1536]{1,0:T(8,128)(2,1)S(1)}, u32[]{:S(2)}, u32[]{:S(2)}) %collective-permute-start.2) | collective-permute-done | bytes 393248 | tf_op jit(solution)/shard_map/ppermute | solution.py:202
  183.9 10.0 %conditional.9 = ((f32[1,1536]{1,0:T(1,128)S(1)}, bf16[128,1536]{1,0:T(8,128)(2,1)})) conditional(s32[]{:T(128)} %convert_element_type.42, (f32[1,1536]{1,0:T(1,128)S(1)}, bf16[128,1536]{1,0:T(8,128)(2,1)}) %tuple.48, (bf16[128,1536]{1,0:T(8,128)(2,1)S(1)}, f32[128,3072]{1,0:T(8,128)S(1)}, f32[128,1536]{1,0:T(8,128)S(1)}, ...), branch_computations={%region_13.14_spmd, %region_14.15_spmd} | conditional | flops 2415919104 | bytes 22806552 | solution.py:198
  183.9 10.0 %branch_1_fun.7 = (bf16[128,1536]{1,0:T(8,128)(2,1)}, f32[1,1536]{1,0:T(1,128)S(1)}) custom-call(bf16[128,1536]{1,0:T(8,128)(2,1)S(1)} %get-tuple-element.95.g_ref, f32[128,3072]{1,0:T(8,128)S(1)} %get-tuple-element.96.act_ref, f32[128,1536]{1,0:T(8,128)S(1)} %get-tuple-element.97.xh_ref, f32[128,128]{1,0:T(8,128)S(1)} %get-tuple-element.98.inv_ref, ...), custom_call_target="tpu_custom_call" | custom-call | flops 2415919104 | bytes 22806528 | tf_op jit(solution)/shard_map/cond/branch_1_fun/pallas_call | solution.py:122
  193.9 2.5 %psum.21 = f32[1,1536]{1,0:T(1,128)S(1)} all-reduce(f32[1,1536]{1,0:T(1,128)S(1)} %get-tuple-element.120), channel_id=1, replica_groups=mesh['segment'=4,'z'=8,'y'=4,'core'=2] {'core'}, use_global_device_ids=true, to_apply=%region_15.16 | all-reduce | flops 1536 | bytes 12288 | tf_op jit(solution)/shard_map/psum | solution.py:203
  196.4 9.7 %psum.22 = f32[1,1536]{1,0:T(1,128)S(1)} all-reduce(f32[1,1536]{1,0:T(1,128)S(1)} %psum.21), channel_id=1, replica_groups=mesh['segment'=4,'z'=8,'y'=4,'core'=2] {'y'}, use_global_device_ids=true, to_apply=%region_16.17 | all-reduce | flops 1536 | bytes 12288 | tf_op jit(solution)/shard_map/psum | solution.py:203
  206.0 16.3 %psum.23 = f32[1,1536]{1,0:T(1,128)} all-reduce(f32[1,1536]{1,0:T(1,128)S(1)} %psum.22), channel_id=1, replica_groups=mesh['segment'=4,'z'=8,'y'=4,'core'=2] {'z'}, use_global_device_ids=true, to_apply=%region_17.18 | all-reduce | flops 1536 | bytes 12288 | tf_op jit(solution)/shard_map/psum | solution.py:203
  (7 shorter events, 0.0 us)
Async XLA Ops:
  7.2 5.6 %copy-start = (bf16[1,128,1536]{2,1,0:T(8,128)(2,1)S(1)}, bf16[1,128,1536]{2,1,0:T(8,128)(2,1)}, u32[]{:S(2)}) copy-start(bf16[1,128,1536]{2,1,0:T(8,128)(2,1)} %param.16) | copy-start | bytes 1179652
  7.2 5.8 %copy-start.1 = (bf16[128,1536]{1,0:T(8,128)(2,1)S(1)}, bf16[128,1536]{1,0:T(8,128)(2,1)}, u32[]{:S(2)}) copy-start(bf16[128,1536]{1,0:T(8,128)(2,1)} %param.20) | copy-start | bytes 1179652
  7.2 110.3 %all-gather.2.cloned.1.call-start = ((), (), s32[]{:S(2)}) async-start(), calls=%async_computation | async-start | bytes 19169280 | tf_op jit(solution)/shard_map/all_gather | solution.py:169
  11.6 106.0 %copy-start.2 = (f32[1,1536]{1,0:T(1,128)S(1)}, f32[1,1536]{1,0:T(1,128)}, u32[]{:S(2)}) copy-start(f32[1,1536]{1,0:T(1,128)} %param.17) | copy-start | bytes 18436
  118.4 6.0 %collective-permute-start = (bf16[128,1536]{1,0:T(8,128)(2,1)}, bf16[128,1536]{1,0:T(8,128)(2,1)S(1)}, u32[]{:S(2)}, u32[]{:S(2)}) collective-permute-start(bf16[128,1536]{1,0:T(8,128)(2,1)} %get-tuple-element.111), channel_id=1, source_target_pairs={{192,128},{193,129},{194,130},{195,131},{196,132},{197,133},{198,1... | collective-permute-start | bytes 1179656 | tf_op jit(solution)/shard_map/ppermute | solution.py:202
  124.4 0.7 collective-permute-start.1
  125.2 58.8 %collective-permute-start.2 = (bf16[128,1536]{1,0:T(8,128)(2,1)}, bf16[128,1536]{1,0:T(8,128)(2,1)S(1)}, u32[]{:S(2)}, u32[]{:S(2)}) collective-permute-start(bf16[128,1536]{1,0:T(8,128)(2,1)} %get-tuple-element.114), channel_id=1, source_target_pairs={{64,0},{65,1},{66,2},{67,3},{68,4},{69,5},{70,6},{71,7},{72,8},{73... | collective-permute-start | bytes 1179656 | tf_op jit(solution)/shard_map/ppermute | solution.py:202
Sparse Core Ops, SparseCore 0:
  11.3 106.1 all-gather.1

commit v5 on v4

--- a/solution.py
+++ b/solution.py
@@ -13,7 +13,7 @@
 def act_kernel(z_ref, w1_ref, act_ref):
     hidden = jnp.dot(z_ref[...], w1_ref[...], preferred_element_type=jnp.float32)
     sig = jax.nn.sigmoid(hidden)
-    act_ref[...] = sig + hidden * sig * (1.0 - sig)
+    act_ref[...] = (sig + hidden * sig * (1.0 - sig)).astype(act_ref.dtype)
 
 
 def hidden_slope(normed, weights):
@@ -27,10 +27,10 @@
             pl.BlockSpec((width, CHUNK), lambda k: (0, k)),
         ],
         out_specs=pl.BlockSpec((rows, CHUNK), lambda k: (0, k)),
-        out_shape=jax.ShapeDtypeStruct((rows, ff), jnp.float32),
+        out_shape=jax.ShapeDtypeStruct((rows, ff), jnp.bfloat16),
         cost_estimate=pl.CostEstimate(
             flops=2 * rows * width * ff, transcendentals=rows * ff,
-            bytes_accessed=2 * width * ff + 4 * rows * ff + 2 * rows * width,
+            bytes_accessed=2 * width * ff + 2 * rows * ff + 2 * rows * width,
         ),
     )(normed, weights)
 
@@ -105,7 +105,7 @@
         acc_ref[...] = jnp.zeros_like(acc_ref)
 
     up_grad = jnp.dot(g_ref[...], w2_ref[...], preferred_element_type=jnp.float32)
-    hid_grad = (0.5 * up_grad * act_ref[...]).astype(jnp.bfloat16)
+    hid_grad = (0.5 * up_grad * act_ref[...].astype(jnp.float32)).astype(jnp.bfloat16)
     acc_ref[...] += lax.dot_general(
         hid_grad, w1_ref[...], (((1,), (1,)), ((), ())), preferred_element_type=jnp.float32
     )
@@ -165,7 +165,11 @@
     standardized_input = centered_input * inverse_deviation
     gain_vector = gains[0]
     normalized_input = (standardized_input * gain_vector).astype(jnp.bfloat16)
-    local = jnp.concatenate([w_in[0], w_out[0].T], axis=1)
+    eye = jnp.eye(w_out.shape[2], dtype=w_out.dtype)
+    w_out_t = lax.dot_general(
+        eye, w_out[0], (((1,), (1,)), ((), ())), preferred_element_type=jnp.float32
+    ).astype(w_out.dtype)
+    local = jnp.concatenate([w_in[0], w_out_t], axis=1)
     weights = lax.all_gather(local, DP, axis=0, tiled=True)
 
     inverse_rows = jnp.broadcast_to(inverse_deviation, (rows, 128))
@@ -175,7 +179,7 @@
     first = segments - 1
     slope = lax.cond(
         my_segment == first,
-        lambda: jnp.zeros((rows, weights.shape[1] // 2), jnp.float32),
+        lambda: jnp.zeros((rows, weights.shape[1] // 2), jnp.bfloat16),
         lambda: hidden_slope(normalized_input, weights),
     )
 

time: 230 us -> 227 us (0.987)
  waiting for transfers between devices: 162 us -> 157 us
    all_gather x1, waiting for transfers between devices: 104 us -> 101 us  [on_device(): weights = lax.all_gather(local, DP, axis=0, tiled=True)]
  transfers between devices with their start and end apart: 4 -> 4, of which waited for: 2 -> 2; matrix products, arithmetic and copies ran while one was open for 2% -> 3% of each run, Pallas kernels for 2% -> 2%
where the time goes in v5:
time: 227 us; the launch traced here: 226 us
  waiting for transfers between devices  157 us (69%)
  blocking collectives  28.4 us (13%)
  Pallas kernels  15.3 us (7%)
  between operations  14.2 us (6%)
  other arithmetic  7.28 us (3%)
  starting transfers between devices  2.7 us (1%)
    all_gather x1, waiting for transfers between devices, on_device(): weights = lax.all_gather(local, DP, axis=0, tiled=True)  101 us
    ppermute x3, waiting for transfers between devices, on_device(): current = lax.ppermute(result, 'segment', [(level, level - 1)])  55.4 us
    psum x3, blocking collectives, on_device(): gain_total = lax.psum(lax.psum(lax.psum(gain_local, 'core'), 'y'), 'z')  28.4 us
    pallas_call x1, Pallas kernels, segment_back(): pl.pallas_call(segment_kernel, grid=(steps,), in_specs=[pl.BlockSpec((row...  9.97 us
    pallas_call x1, Pallas kernels, hidden_slope(): pl.pallas_call(act_kernel, grid=(ff // CHUNK,), in_specs=[pl.BlockSpec((r...  5.3 us
  transfers between devices with their start and end apart: 4, of which 2 were waited for; matrix products, arithmetic and copies ran while one was open for 3% of the time, Pallas kernels for 2%

profile of v5, /device:TPU:8, one launch (start us, length us, event | category | flops | bytes accessed | tf_op | source)
XLA Modules:
  0.0 226.4 jit_solution(9827956477734502685)
XLA Ops:
  7.2 0.0 copy-start
  7.2 0.0 all-gather.2.cloned.1.call-start
  7.2 0.9 copy-done
  8.1 0.2 convolution_convert_fusion
  8.3 1.7 pad_maximum_fusion
  9.9 0.0 all-gather.2.cloned.1.call-update
  9.9 0.7 copy.10
  10.7 0.1 reduce-window.8
  10.8 0.1 reduce.1
  10.9 0.7 reduce.2
  11.6 0.1 convert_reduce_fusion.1
  11.7 0.7 select_reduce_fusion
  12.5 1.1 convert_reduce_fusion
  13.6 1.2 fusion.3
  14.9 1.5 fusion.1
  16.4 101.2 %all-gather.2.cloned.1.call-done = bf16[1536,6144]{1,0:T(8,128)(2,1)} async-done(((bf16[24,6144]{1,0:T(8,128)(2,1)}), bf16[1536,6144]{1,0:T(8,128)(2,1)}) %all-gather.2.cloned.1.call-update) | async-done | bytes 18874384 | tf_op jit(solution)/shard_map/all_gather | solution.py:173
  117.5 0.1 broadcast_in_dim.9
  117.6 0.1 conditional.5
  117.7 0.0 copy-start.2
  117.7 0.7 collective-permute-start
  118.4 5.3 %conditional.6 = (bf16[128,3072]{1,0:T(8,128)(2,1)S(1)}) conditional(s32[]{:T(128)} %convert_element_type.49, (bf16[128,1536]{1,0:T(8,128)(2,1)S(1)}, bf16[1536,6144]{1,0:T(8,128)(2,1)}) %tuple.44, () %tuple.45), branch_computations={%region_7.8_spmd, %region_8.9_spmd} | conditional | flops 1207959552 | bytes 10616840 | solution.py:180
  118.4 5.3 %branch_0_fun.1 = bf16[128,3072]{1,0:T(8,128)(2,1)S(1)} custom-call(bf16[128,1536]{1,0:T(8,128)(2,1)S(1)} %get-tuple-element.81.z_ref, bf16[1536,6144]{1,0:T(8,128)(2,1)} %get-tuple-element.82.w1_ref), custom_call_target="tpu_custom_call" | custom-call | flops 1207959552 | bytes 10616832 | tf_op jit(solution)/shard_map/cond/branch_0_fun/pallas_call | solution.py:22
  123.7 0.0 collective-permute-done
  123.7 0.0 copy-done.2
  123.7 0.7 collective-permute-start.1
  124.4 0.0 collective-permute-done.1
  124.5 0.0 copy-start.1
  124.5 1.3 collective-permute-start.2
  125.8 55.4 %collective-permute-done.2 = bf16[128,1536]{1,0:T(8,128)(2,1)S(1)} collective-permute-done((bf16[128,1536]{1,0:T(8,128)(2,1)S(1)}, bf16[128,1536]{1,0:T(8,128)(2,1)S(1)}, u32[]{:S(2)}, u32[]{:S(2)}) %collective-permute-start.2) | collective-permute-done | bytes 393248 | tf_op jit(solution)/shard_map/ppermute | solution.py:206
  181.1 0.0 copy-done.1
  181.2 10.0 %conditional.9 = (f32[1,1536]{1,0:T(1,128)S(1)}, bf16[1,128,1536]{2,1,0:T(8,128)(2,1)}) conditional(s32[]{:T(128)} %convert_element_type.46, (f32[1,1536]{1,0:T(1,128)S(1)}, bf16[128,1536]{1,0:T(8,128)(2,1)}) %tuple.74, (bf16[128,1536]{1,0:T(8,128)(2,1)S(1)}, bf16[128,3072]{1,0:T(8,128)(2,1)S(1)}, f32[128,1536]{1,0:T(8,128)S(1)}, ...), branch_computations={%region_13.14_spmd, %region_14.15_spmd} | conditional | flops 2415919104 | bytes 22806544 | solution.py:202
  181.2 10.0 %branch_1_fun.7 = (bf16[128,1536]{1,0:T(8,128)(2,1)}, f32[1,1536]{1,0:T(1,128)S(1)}) custom-call(bf16[128,1536]{1,0:T(8,128)(2,1)S(1)} %get-tuple-element.95.g_ref, bf16[128,3072]{1,0:T(8,128)(2,1)S(1)} %get-tuple-element.96.act_ref, f32[128,1536]{1,0:T(8,128)S(1)} %get-tuple-element.97.xh_ref, f32[128,128]{1,0:T(8,128)S(1)} %get-tuple-element.98.inv_ref, ...), custom_call_target="tpu_custom_call" | custom-call | flops 2415919104 | bytes 22806528 | tf_op jit(solution)/shard_map/cond/branch_1_fun/pallas_call | solution.py:122
  191.1 2.5 %psum.21 = f32[1,1536]{1,0:T(1,128)S(1)} all-reduce(f32[1,1536]{1,0:T(1,128)S(1)} %get-tuple-element.116), channel_id=1, replica_groups=mesh['segment'=4,'z'=8,'y'=4,'core'=2] {'core'}, use_global_device_ids=true, to_apply=%region_15.16 | all-reduce | flops 1536 | bytes 12288 | tf_op jit(solution)/shard_map/psum | solution.py:207
  193.6 9.6 %psum.22 = f32[1,1536]{1,0:T(1,128)S(1)} all-reduce(f32[1,1536]{1,0:T(1,128)S(1)} %psum.21), channel_id=1, replica_groups=mesh['segment'=4,'z'=8,'y'=4,'core'=2] {'y'}, use_global_device_ids=true, to_apply=%region_16.17 | all-reduce | flops 1536 | bytes 12288 | tf_op jit(solution)/shard_map/psum | solution.py:207
  203.2 16.3 %psum.23 = f32[1,1536]{1,0:T(1,128)} all-reduce(f32[1,1536]{1,0:T(1,128)S(1)} %psum.22), channel_id=1, replica_groups=mesh['segment'=4,'z'=8,'y'=4,'core'=2] {'z'}, use_global_device_ids=true, to_apply=%region_17.18 | all-reduce | flops 1536 | bytes 12288 | tf_op jit(solution)/shard_map/psum | solution.py:207
  (8 shorter events, 0.1 us)
Async XLA Ops:
  7.2 0.9 copy-start
  7.2 110.3 %all-gather.2.cloned.1.call-start = ((), (), s32[]{:S(2)}) async-start(), calls=%async_computation | async-start | bytes 19169280 | tf_op jit(solution)/shard_map/all_gather | solution.py:173
  117.7 6.1 %copy-start.2 = (f32[1,1536]{1,0:T(1,128)S(1)}, f32[1,1536]{1,0:T(1,128)}, u32[]{:S(2)}) copy-start(f32[1,1536]{1,0:T(1,128)} %param.17) | copy-start | bytes 18436
  117.7 6.0 %collective-permute-start = (bf16[128,1536]{1,0:T(8,128)(2,1)S(1)}, bf16[128,1536]{1,0:T(8,128)(2,1)S(1)}, u32[]{:S(2)}, u32[]{:S(2)}) collective-permute-start(bf16[128,1536]{1,0:T(8,128)(2,1)S(1)} %get-tuple-element.111), channel_id=1, source_target_pairs={{192,128},{193,129},{194,130},{195,131},{196,132},{197,133},{198,1... | collective-permute-start | bytes 1179656 | tf_op jit(solution)/shard_map/ppermute | solution.py:206
  123.7 0.7 collective-permute-start.1
  124.5 56.7 %copy-start.1 = (bf16[128,1536]{1,0:T(8,128)(2,1)}, bf16[128,1536]{1,0:T(8,128)(2,1)S(1)}, u32[]{:S(2)}) copy-start(bf16[128,1536]{1,0:T(8,128)(2,1)S(1)} %get-tuple-element.140) | copy-start | bytes 1179652
  124.5 56.7 %collective-permute-start.2 = (bf16[128,1536]{1,0:T(8,128)(2,1)S(1)}, bf16[128,1536]{1,0:T(8,128)(2,1)S(1)}, u32[]{:S(2)}, u32[]{:S(2)}) collective-permute-start(bf16[128,1536]{1,0:T(8,128)(2,1)S(1)} %get-tuple-element.140), channel_id=1, source_target_pairs={{64,0},{65,1},{66,2},{67,3},{68,4},{69,5},{70,6},{71,7},{72,8},{73... | collective-permute-start | bytes 1179656 | tf_op jit(solution)/shard_map/ppermute | solution.py:206
Sparse Core Ops, SparseCore 0:
  11.3 106.1 all-gather.1

commit v6 on v5

--- a/solution.py
+++ b/solution.py
@@ -165,11 +165,7 @@
     standardized_input = centered_input * inverse_deviation
     gain_vector = gains[0]
     normalized_input = (standardized_input * gain_vector).astype(jnp.bfloat16)
-    eye = jnp.eye(w_out.shape[2], dtype=w_out.dtype)
-    w_out_t = lax.dot_general(
-        eye, w_out[0], (((1,), (1,)), ((), ())), preferred_element_type=jnp.float32
-    ).astype(w_out.dtype)
-    local = jnp.concatenate([w_in[0], w_out_t], axis=1)
+    local = jnp.concatenate([w_in[0], w_out[0].T], axis=1)
     weights = lax.all_gather(local, DP, axis=0, tiled=True)
 
     inverse_rows = jnp.broadcast_to(inverse_deviation, (rows, 128))

time: 227 us -> 227 us (level)
  no operation moved by 1% of the time
where the time goes in v6:
time: 227 us; the launch traced here: 226 us
  waiting for transfers between devices  158 us (70%)
  blocking collectives  28.4 us (13%)
  Pallas kernels  15.3 us (7%)
  between operations  14.2 us (6%)
  other arithmetic  7.35 us (3%)
  starting transfers between devices  2.7 us (1%)
    all_gather x1, waiting for transfers between devices, on_device(): weights = lax.all_gather(local, DP, axis=0, tiled=True)  102 us
    ppermute x3, waiting for transfers between devices, on_device(): current = lax.ppermute(result, 'segment', [(level, level - 1)])  55.4 us
    psum x3, blocking collectives, on_device(): gain_total = lax.psum(lax.psum(lax.psum(gain_local, 'core'), 'y'), 'z')  28.4 us
    pallas_call x1, Pallas kernels, segment_back(): pl.pallas_call(segment_kernel, grid=(steps,), in_specs=[pl.BlockSpec((row...  9.97 us
    pallas_call x1, Pallas kernels, hidden_slope(): pl.pallas_call(act_kernel, grid=(ff // CHUNK,), in_specs=[pl.BlockSpec((r...  5.3 us
  transfers between devices with their start and end apart: 4, of which 2 were waited for; matrix products, arithmetic and copies ran while one was open for 3% of the time, Pallas kernels for 2%

profile of v6, /device:TPU:8, one launch (start us, length us, event | category | flops | bytes accessed | tf_op | source)
XLA Modules:
  0.0 226.4 jit_solution(15251340594415415271)
XLA Ops:
  7.2 0.0 all-gather.2.cloned.1.call-start
  7.2 1.7 pad_maximum_fusion
  8.9 0.0 all-gather.2.cloned.1.call-update
  9.0 0.7 copy.10
  9.7 0.1 reduce-window.8
  9.8 0.1 reduce.1
  9.9 0.7 reduce.2
  10.7 0.1 convert_reduce_fusion.1
  10.8 0.7 select_reduce_fusion
  11.5 1.1 convert_reduce_fusion
  12.6 1.2 fusion.3
  13.9 1.5 fusion.1
  15.4 102.1 %all-gather.2.cloned.1.call-done = bf16[1536,6144]{1,0:T(8,128)(2,1)} async-done(((bf16[24,6144]{1,0:T(8,128)(2,1)}), bf16[1536,6144]{1,0:T(8,128)(2,1)}) %all-gather.2.cloned.1.call-update) | async-done | bytes 18874384 | tf_op jit(solution)/shard_map/all_gather | solution.py:169
  117.5 0.1 broadcast_in_dim.9
  117.6 0.1 conditional.5
  117.6 0.0 copy-start.1
  117.7 0.7 collective-permute-start
  118.4 5.3 %conditional.6 = (bf16[128,3072]{1,0:T(8,128)(2,1)S(1)}) conditional(s32[]{:T(128)} %convert_element_type.45, (bf16[128,1536]{1,0:T(8,128)(2,1)S(1)}, bf16[1536,6144]{1,0:T(8,128)(2,1)}) %tuple.44, () %tuple.45), branch_computations={%region_7.8_spmd, %region_8.9_spmd} | conditional | flops 1207959552 | bytes 10616840 | solution.py:176
  118.4 5.3 %branch_0_fun.1 = bf16[128,3072]{1,0:T(8,128)(2,1)S(1)} custom-call(bf16[128,1536]{1,0:T(8,128)(2,1)S(1)} %get-tuple-element.81.z_ref, bf16[1536,6144]{1,0:T(8,128)(2,1)} %get-tuple-element.82.w1_ref), custom_call_target="tpu_custom_call" | custom-call | flops 1207959552 | bytes 10616832 | tf_op jit(solution)/shard_map/cond/branch_0_fun/pallas_call | solution.py:22
  123.7 0.0 collective-permute-done
  123.7 0.0 copy-done.1
  123.7 0.7 collective-permute-start.1
  124.4 0.0 collective-permute-done.1
  124.5 0.0 copy-start
  124.5 1.3 collective-permute-start.2
  125.8 55.4 %collective-permute-done.2 = bf16[128,1536]{1,0:T(8,128)(2,1)S(1)} collective-permute-done((bf16[128,1536]{1,0:T(8,128)(2,1)S(1)}, bf16[128,1536]{1,0:T(8,128)(2,1)S(1)}, u32[]{:S(2)}, u32[]{:S(2)}) %collective-permute-start.2) | collective-permute-done | bytes 393248 | tf_op jit(solution)/shard_map/ppermute | solution.py:202
  181.1 0.0 copy-done
  181.1 10.0 %conditional.9 = ((f32[1,1536]{1,0:T(1,128)S(1)}, bf16[128,1536]{1,0:T(8,128)(2,1)})) conditional(s32[]{:T(128)} %convert_element_type.42, (f32[1,1536]{1,0:T(1,128)S(1)}, bf16[128,1536]{1,0:T(8,128)(2,1)}) %tuple.78, (bf16[128,1536]{1,0:T(8,128)(2,1)S(1)}, bf16[128,3072]{1,0:T(8,128)(2,1)S(1)}, f32[128,1536]{1,0:T(8,128)S(1)}, ...), branch_computations={%region_13.14_spmd, %region_14.15_spmd} | conditional | flops 2415919104 | bytes 22806552 | solution.py:198
  181.1 10.0 %branch_1_fun.7 = (bf16[128,1536]{1,0:T(8,128)(2,1)}, f32[1,1536]{1,0:T(1,128)S(1)}) custom-call(bf16[128,1536]{1,0:T(8,128)(2,1)S(1)} %get-tuple-element.95.g_ref, bf16[128,3072]{1,0:T(8,128)(2,1)S(1)} %get-tuple-element.96.act_ref, f32[128,1536]{1,0:T(8,128)S(1)} %get-tuple-element.97.xh_ref, f32[128,128]{1,0:T(8,128)S(1)} %get-tuple-element.98.inv_ref, ...), custom_call_target="tpu_custom_call" | custom-call | flops 2415919104 | bytes 22806528 | tf_op jit(solution)/shard_map/cond/branch_1_fun/pallas_call | solution.py:122
  191.1 2.5 %psum.21 = f32[1,1536]{1,0:T(1,128)S(1)} all-reduce(f32[1,1536]{1,0:T(1,128)S(1)} %get-tuple-element.120), channel_id=1, replica_groups=mesh['segment'=4,'z'=8,'y'=4,'core'=2] {'core'}, use_global_device_ids=true, to_apply=%region_15.16 | all-reduce | flops 1536 | bytes 12288 | tf_op jit(solution)/shard_map/psum | solution.py:203
  193.6 9.6 %psum.22 = f32[1,1536]{1,0:T(1,128)S(1)} all-reduce(f32[1,1536]{1,0:T(1,128)S(1)} %psum.21), channel_id=1, replica_groups=mesh['segment'=4,'z'=8,'y'=4,'core'=2] {'y'}, use_global_device_ids=true, to_apply=%region_16.17 | all-reduce | flops 1536 | bytes 12288 | tf_op jit(solution)/shard_map/psum | solution.py:203
  203.2 16.3 %psum.23 = f32[1,1536]{1,0:T(1,128)} all-reduce(f32[1,1536]{1,0:T(1,128)S(1)} %psum.22), channel_id=1, replica_groups=mesh['segment'=4,'z'=8,'y'=4,'core'=2] {'z'}, use_global_device_ids=true, to_apply=%region_17.18 | all-reduce | flops 1536 | bytes 12288 | tf_op jit(solution)/shard_map/psum | solution.py:203
  (8 shorter events, 0.1 us)
Async XLA Ops:
  7.2 110.3 %all-gather.2.cloned.1.call-start = ((), (), s32[]{:S(2)}) async-start(), calls=%async_computation | async-start | bytes 19169280 | tf_op jit(solution)/shard_map/all_gather | solution.py:169
  117.6 6.1 %copy-start.1 = (f32[1,1536]{1,0:T(1,128)S(1)}, f32[1,1536]{1,0:T(1,128)}, u32[]{:S(2)}) copy-start(f32[1,1536]{1,0:T(1,128)} %param.17) | copy-start | bytes 18436
  117.7 6.0 %collective-permute-start = (bf16[128,1536]{1,0:T(8,128)(2,1)S(1)}, bf16[128,1536]{1,0:T(8,128)(2,1)S(1)}, u32[]{:S(2)}, u32[]{:S(2)}) collective-permute-start(bf16[128,1536]{1,0:T(8,128)(2,1)S(1)} %get-tuple-element.111), channel_id=1, source_target_pairs={{192,128},{193,129},{194,130},{195,131},{196,132},{197,133},{198,1... | collective-permute-start | bytes 1179656 | tf_op jit(solution)/shard_map/ppermute | solution.py:202
  123.7 0.7 collective-permute-start.1
  124.5 56.7 %copy-start = (bf16[128,1536]{1,0:T(8,128)(2,1)}, bf16[128,1536]{1,0:T(8,128)(2,1)S(1)}, u32[]{:S(2)}) copy-start(bf16[128,1536]{1,0:T(8,128)(2,1)S(1)} %get-tuple-element.114) | copy-start | bytes 1179652
  124.5 56.7 %collective-permute-start.2 = (bf16[128,1536]{1,0:T(8,128)(2,1)S(1)}, bf16[128,1536]{1,0:T(8,128)(2,1)S(1)}, u32[]{:S(2)}, u32[]{:S(2)}) collective-permute-start(bf16[128,1536]{1,0:T(8,128)(2,1)S(1)} %get-tuple-element.114), channel_id=1, source_target_pairs={{64,0},{65,1},{66,2},{67,3},{68,4},{69,5},{70,6},{71,7},{72,8},{73... | collective-permute-start | bytes 1179656 | tf_op jit(solution)/shard_map/ppermute | solution.py:202
Sparse Core Ops, SparseCore 0:
  11.3 106.1 all-gather.1

commit v7 on v6

--- a/solution.py
+++ b/solution.py
@@ -35,12 +35,15 @@
     )(normed, weights)
 
 
-def fused_kernel(z_ref, g_ref, xh_ref, inv_ref, gain_ref, w1_ref, w2_ref, out_ref, gp_ref, acc_ref):
+def fused_kernel(
+    x_ref, g_ref, mean_ref, inv_ref, gain_ref, w1_ref, w2_ref, out_ref, gp_ref, acc_ref, z_ref
+):
     k = pl.program_id(0)
 
     @pl.when(k == 0)
     def _():
         acc_ref[...] = jnp.zeros_like(acc_ref)
+        z_ref[...] = (standardize(x_ref, mean_ref, inv_ref) * gain_ref[...]).astype(z_ref.dtype)
 
     w1 = w1_ref[...]
     hidden = jnp.dot(z_ref[...], w1, preferred_element_type=jnp.float32)
@@ -53,12 +56,16 @@
 
     @pl.when(k == pl.num_programs(0) - 1)
     def _():
-        norm_backward(acc_ref, xh_ref, inv_ref, gain_ref, g_ref, out_ref, gp_ref)
-
-
-def norm_backward(acc_ref, xh_ref, inv_ref, gain_ref, g_ref, out_ref, gp_ref):
+        norm_backward(acc_ref, x_ref, mean_ref, inv_ref, gain_ref, g_ref, out_ref, gp_ref)
+
+
+def standardize(x_ref, mean_ref, inv_ref):
+    return (x_ref[...].astype(jnp.float32) - mean_ref[:, 0:1]) * inv_ref[:, 0:1]
+
+
+def norm_backward(acc_ref, x_ref, mean_ref, inv_ref, gain_ref, g_ref, out_ref, gp_ref):
     norm_gradient = acc_ref[...]
-    standardized = xh_ref[...]
+    standardized = standardize(x_ref, mean_ref, inv_ref)
     gp_ref[...] = jnp.sum(norm_gradient * standardized, axis=0, keepdims=True)
     gain_scaled = norm_gradient * gain_ref[...]
     mean_e = jnp.mean(gain_scaled, axis=-1, keepdims=True)
@@ -67,8 +74,8 @@
     out_ref[...] = (g_ref[...].astype(jnp.float32) + back).astype(out_ref.dtype)
 
 
-def fused_back(normed, grad_in, standardized, inverse_deviation, gain_row, weights):
-    rows, width = normed.shape
+def fused_back(saved, grad_in, mean_rows, inverse_deviation, gain_row, weights):
+    rows, width = saved.shape
     steps = weights.shape[1] // 2 // CHUNK
     whole = lambda k: (0, 0)
     return pl.pallas_call(
@@ -77,7 +84,7 @@
         in_specs=[
             pl.BlockSpec((rows, width), whole),
             pl.BlockSpec((rows, width), whole),
-            pl.BlockSpec((rows, width), whole),
+            pl.BlockSpec(mean_rows.shape, whole),
             pl.BlockSpec(inverse_deviation.shape, whole),
             pl.BlockSpec((1, width), whole),
             pl.BlockSpec((width, CHUNK), lambda k: (0, k)),
@@ -88,16 +95,21 @@
             jax.ShapeDtypeStruct((rows, width), jnp.bfloat16),
             jax.ShapeDtypeStruct((1, width), jnp.float32),
         ],
-        scratch_shapes=[pltpu.VMEM((rows, width), jnp.float32)],
+        scratch_shapes=[
+            pltpu.VMEM((rows, width), jnp.float32),
+            pltpu.VMEM((rows, width), jnp.bfloat16),
+        ],
         cost_estimate=pl.CostEstimate(
             flops=6 * rows * width * weights.shape[1] // 2,
             transcendentals=rows * weights.shape[1] // 2,
             bytes_accessed=2 * weights.size + 12 * rows * width,
         ),
-    )(normed, grad_in, standardized, inverse_deviation, gain_row, weights, weights)
-
-
-def segment_kernel(g_ref, act_ref, xh_ref, inv_ref, gain_ref, w1_ref, w2_ref, out_ref, gp_ref, acc_ref):
+    )(saved, grad_in, mean_rows, inverse_deviation, gain_row, weights, weights)
+
+
+def segment_kernel(
+    g_ref, act_ref, x_ref, mean_ref, inv_ref, gain_ref, w1_ref, w2_ref, out_ref, gp_ref, acc_ref
+):
     k = pl.program_id(0)
 
     @pl.when(k == 0)
@@ -112,10 +124,10 @@
 
     @pl.when(k == pl.num_programs(0) - 1)
     def _():
-        norm_backward(acc_ref, xh_ref, inv_ref, gain_ref, g_ref, out_ref, gp_ref)
-
-
-def segment_back(grad_in, slope, standardized, inverse_deviation, gain_row, weights):
+        norm_backward(acc_ref, x_ref, mean_ref, inv_ref, gain_ref, g_ref, out_ref, gp_ref)
+
+
+def segment_back(grad_in, slope, saved, mean_rows, inverse_deviation, gain_row, weights):
     rows, width = grad_in.shape
     steps = weights.shape[1] // 2 // CHUNK
     whole = lambda k: (0, 0)
@@ -126,6 +138,7 @@
             pl.BlockSpec((rows, width), whole),
             pl.BlockSpec((rows, CHUNK), lambda k: (0, k)),
             pl.BlockSpec((rows, width), whole),
+            pl.BlockSpec(mean_rows.shape, whole),
             pl.BlockSpec(inverse_deviation.shape, whole),
             pl.BlockSpec((1, width), whole),
             pl.BlockSpec((width, CHUNK), lambda k: (0, k)),
@@ -142,7 +155,7 @@
             transcendentals=0,
             bytes_accessed=2 * weights.size + 2 * rows * weights.shape[1] + 12 * rows * width,
         ),
-    )(grad_in, slope, standardized, inverse_deviation, gain_row, weights, weights)
+    )(grad_in, slope, saved, mean_rows, inverse_deviation, gain_row, weights, weights)
 
 
 def on_device(x_saved, gains, w_in, w_out, cotangent, lengths):
@@ -159,7 +172,8 @@
     weight = 2.0 * rows / (tok_len + rows)
     current = (cotangent.astype(jnp.float32) * weight[:, None]).astype(jnp.bfloat16)
     xf = x_saved[0].astype(jnp.float32)
-    centered_input = xf - jnp.mean(xf, -1, keepdims=True)
+    mean_input = jnp.mean(xf, -1, keepdims=True)
+    centered_input = xf - mean_input
     variance = jnp.mean(centered_input * centered_input, -1, keepdims=True)
     inverse_deviation = lax.rsqrt(variance + 1e-05)
     standardized_input = centered_input * inverse_deviation
@@ -169,6 +183,7 @@
     weights = lax.all_gather(local, DP, axis=0, tiled=True)
 
     inverse_rows = jnp.broadcast_to(inverse_deviation, (rows, 128))
+    mean_rows = jnp.broadcast_to(mean_input, (rows, 128))
     gain_row = gain_vector[None, :]
     segments = lax.axis_size("segment")
     my_segment = lax.axis_index("segment")
@@ -188,12 +203,12 @@
         if level == first:
             def mine(grad_in, kept, kept_gain):
                 return fused_back(
-                    normalized_input, grad_in, standardized_input, inverse_rows, gain_row, weights
+                    x_saved[0], grad_in, mean_rows, inverse_rows, gain_row, weights
                 )
         else:
             def mine(grad_in, kept, kept_gain):
                 return segment_back(
-                    grad_in, slope, standardized_input, inverse_rows, gain_row, weights
+                    grad_in, slope, x_saved[0], mean_rows, inverse_rows, gain_row, weights
                 )
         result, gain_local = lax.cond(
             my_segment == level, mine, keep, current, result, gain_local

time: 227 us -> 228 us (level)
    convert_element_type x0 -> x2, other arithmetic: none -> 2.41 us  [the longest x1 1.27 us: on_device(): normalized_input = (standardized_input * gain_vector).astype(jnp.bfloat16)]
where the time goes in v7:
time: 228 us
  waiting for transfers between devices  158 us (69%)
  blocking collectives  28.4 us (12%)
  Pallas kernels  15.4 us (7%)
  between operations  14.2 us (6%)
  other arithmetic  8.29 us (4%)
  starting transfers between devices  2.83 us (1%)
    all_gather x1, waiting for transfers between devices, on_device(): weights = lax.all_gather(local, DP, axis=0, tiled=True)  102 us
    ppermute x3, waiting for transfers between devices, on_device(): current = lax.ppermute(result, 'segment', [(level, level - 1)])  55.5 us
    psum x3, blocking collectives, on_device(): gain_total = lax.psum(lax.psum(lax.psum(gain_local, 'core'), 'y'), 'z')  28.4 us
    pallas_call x1, Pallas kernels, segment_back(): pl.pallas_call(segment_kernel, grid=(steps,), in_specs=[pl.BlockSpec((row...  10 us
    pallas_call x1, Pallas kernels, hidden_slope(): pl.pallas_call(act_kernel, grid=(ff // CHUNK,), in_specs=[pl.BlockSpec((r...  5.3 us
  transfers between devices with their start and end apart: 4, of which 2 were waited for; matrix products, arithmetic and copies ran while one was open for 3% of the time, Pallas kernels for 2%

profile of v7, /device:TPU:8, one launch (start us, length us, event | category | flops | bytes accessed | tf_op | source)
XLA Modules:
  0.0 228.0 jit_solution(15207202349365455371)
XLA Ops:
  7.2 0.0 all-gather.2.cloned.1.call-start
  7.2 1.7 pad_maximum_fusion
  8.9 0.0 all-gather.2.cloned.1.call-update
  9.0 0.7 copy.10
  9.7 0.1 reduce-window.8
  9.8 0.1 reduce.1
  9.9 0.7 reduce.2
  10.7 0.1 convert_reduce_fusion.1
  10.8 0.7 select_reduce_fusion
  11.5 1.1 convert_reduce_fusion
  12.6 1.2 fusion.3
  13.9 1.1 multiply_convert_fusion
  15.0 102.5 %all-gather.2.cloned.1.call-done = bf16[1536,6144]{1,0:T(8,128)(2,1)} async-done(((bf16[24,6144]{1,0:T(8,128)(2,1)}), bf16[1536,6144]{1,0:T(8,128)(2,1)}) %all-gather.2.cloned.1.call-update) | async-done | bytes 18874384 | tf_op jit(solution)/shard_map/all_gather | solution.py:183
  117.5 0.1 broadcast_in_dim.12
  117.6 0.1 broadcast_in_dim.11
  117.7 0.0 copy-start
  117.7 0.0 copy-start.2
  117.7 0.8 collective-permute-start
  118.5 1.3 fusion.5
  119.8 5.3 %conditional.6 = (bf16[128,3072]{1,0:T(8,128)(2,1)S(1)}) conditional(s32[]{:T(128)} %convert_element_type.45, (bf16[128,1536]{1,0:T(8,128)(2,1)S(1)}, bf16[1536,6144]{1,0:T(8,128)(2,1)}) %tuple.44, () %tuple.45), branch_computations={%region_7.8_spmd, %region_8.9_spmd} | conditional | flops 1207959552 | bytes 10616840 | solution.py:191
  119.8 5.3 %branch_0_fun.1 = bf16[128,3072]{1,0:T(8,128)(2,1)S(1)} custom-call(bf16[128,1536]{1,0:T(8,128)(2,1)S(1)} %get-tuple-element.87.z_ref, bf16[1536,6144]{1,0:T(8,128)(2,1)} %get-tuple-element.88.w1_ref), custom_call_target="tpu_custom_call" | custom-call | flops 1207959552 | bytes 10616832 | tf_op jit(solution)/shard_map/cond/branch_0_fun/pallas_call | solution.py:22
  125.2 0.0 collective-permute-done
  125.2 0.0 copy-done
  125.2 0.0 copy-done.2
  125.2 0.7 collective-permute-start.1
  125.9 0.0 collective-permute-done.1
  125.9 0.0 copy-start.1
  125.9 1.3 collective-permute-start.2
  127.2 55.5 %collective-permute-done.2 = bf16[128,1536]{1,0:T(8,128)(2,1)S(1)} collective-permute-done((bf16[128,1536]{1,0:T(8,128)(2,1)S(1)}, bf16[128,1536]{1,0:T(8,128)(2,1)S(1)}, u32[]{:S(2)}, u32[]{:S(2)}) %collective-permute-start.2) | collective-permute-done | bytes 393248 | tf_op jit(solution)/shard_map/ppermute | solution.py:217
  182.7 0.0 copy-done.1
  182.7 10.0 %conditional.9 = ((f32[1,1536]{1,0:T(1,128)S(1)}, bf16[128,1536]{1,0:T(8,128)(2,1)})) conditional(s32[]{:T(128)} %convert_element_type.42, (f32[1,1536]{1,0:T(1,128)S(1)}, bf16[128,1536]{1,0:T(8,128)(2,1)}) %tuple.79, (bf16[1,128,1536]{2,1,0:T(8,128)(2,1)S(1)}, bf16[128,1536]{1,0:T(8,128)(2,1)S(1)}, bf16[128,3072]{1,0:T(8,128)(2,1)S(1)}, ...), branch_computations={%region_13.14_spmd, %region_14.15_spmd} | conditional | flops 2415919104 | bytes 22806552 | solution.py:213
  182.7 10.0 %branch_1_fun.7 = (bf16[128,1536]{1,0:T(8,128)(2,1)}, f32[1,1536]{1,0:T(1,128)S(1)}) custom-call(bf16[128,1536]{1,0:T(8,128)(2,1)S(1)} %get-tuple-element.103.g_ref, bf16[128,3072]{1,0:T(8,128)(2,1)S(1)} %get-tuple-element.104.act_ref, bf16[128,1536]{1,0:T(8,128)(2,1)S(1)} %bitcast.27, f32[128,128]{1,0:T(8,128)S(1)} %get-tuple-element.106.mean_ref, ...), custom_call_target="tpu_custom_call" | custom-call | flops 2415919104 | bytes 22806528 | tf_op jit(solution)/shard_map/cond/branch_1_fun/pallas_call | solution.py:134
  192.8 2.5 %psum.21 = f32[1,1536]{1,0:T(1,128)S(1)} all-reduce(f32[1,1536]{1,0:T(1,128)S(1)} %get-tuple-element.129), channel_id=1, replica_groups=mesh['segment'=4,'z'=8,'y'=4,'core'=2] {'core'}, use_global_device_ids=true, to_apply=%region_15.16 | all-reduce | flops 1536 | bytes 12288 | tf_op jit(solution)/shard_map/psum | solution.py:218
  195.2 9.6 %psum.22 = f32[1,1536]{1,0:T(1,128)S(1)} all-reduce(f32[1,1536]{1,0:T(1,128)S(1)} %psum.21), channel_id=1, replica_groups=mesh['segment'=4,'z'=8,'y'=4,'core'=2] {'y'}, use_global_device_ids=true, to_apply=%region_16.17 | all-reduce | flops 1536 | bytes 12288 | tf_op jit(solution)/shard_map/psum | solution.py:218
  204.9 16.3 %psum.23 = f32[1,1536]{1,0:T(1,128)} all-reduce(f32[1,1536]{1,0:T(1,128)S(1)} %psum.22), channel_id=1, replica_groups=mesh['segment'=4,'z'=8,'y'=4,'core'=2] {'z'}, use_global_device_ids=true, to_apply=%region_17.18 | all-reduce | flops 1536 | bytes 12288 | tf_op jit(solution)/shard_map/psum | solution.py:218
  (8 shorter events, 0.1 us)
Async XLA Ops:
  7.2 110.3 %all-gather.2.cloned.1.call-start = ((), (), s32[]{:S(2)}) async-start(), calls=%async_computation | async-start | bytes 19169280 | tf_op jit(solution)/shard_map/all_gather | solution.py:183
  117.7 7.5 %copy-start = (bf16[1,128,1536]{2,1,0:T(8,128)(2,1)S(1)}, bf16[1,128,1536]{2,1,0:T(8,128)(2,1)}, u32[]{:S(2)}) copy-start(bf16[1,128,1536]{2,1,0:T(8,128)(2,1)} %param.16) | copy-start | bytes 1179652
  117.7 7.5 %copy-start.2 = (f32[1,1536]{1,0:T(1,128)S(1)}, f32[1,1536]{1,0:T(1,128)}, u32[]{:S(2)}) copy-start(f32[1,1536]{1,0:T(1,128)} %param.17) | copy-start | bytes 18436
  117.7 7.4 %collective-permute-start = (bf16[128,1536]{1,0:T(8,128)(2,1)S(1)}, bf16[128,1536]{1,0:T(8,128)(2,1)S(1)}, u32[]{:S(2)}, u32[]{:S(2)}) collective-permute-start(bf16[128,1536]{1,0:T(8,128)(2,1)S(1)} %get-tuple-element.120), channel_id=1, source_target_pairs={{192,128},{193,129},{194,130},{195,131},{196,132},{197,133},{198,1... | collective-permute-start | bytes 1179656 | tf_op jit(solution)/shard_map/ppermute | solution.py:217
  125.2 0.7 collective-permute-start.1
  125.9 56.8 %copy-start.1 = (bf16[128,1536]{1,0:T(8,128)(2,1)}, bf16[128,1536]{1,0:T(8,128)(2,1)S(1)}, u32[]{:S(2)}) copy-start(bf16[128,1536]{1,0:T(8,128)(2,1)S(1)} %get-tuple-element.123) | copy-start | bytes 1179652
  125.9 56.8 %collective-permute-start.2 = (bf16[128,1536]{1,0:T(8,128)(2,1)S(1)}, bf16[128,1536]{1,0:T(8,128)(2,1)S(1)}, u32[]{:S(2)}, u32[]{:S(2)}) collective-permute-start(bf16[128,1536]{1,0:T(8,128)(2,1)S(1)} %get-tuple-element.123), channel_id=1, source_target_pairs={{64,0},{65,1},{66,2},{67,3},{68,4},{69,5},{70,6},{71,7},{72,8},{73... | collective-permute-start | bytes 1179656 | tf_op jit(solution)/shard_map/ppermute | solution.py:217
Sparse Core Ops, SparseCore 0:
  11.3 106.1 all-gather.1

commit v8 on v6

--- a/solution.py
+++ b/solution.py
@@ -18,13 +18,13 @@
 
 def hidden_slope(normed, weights):
     rows, width = normed.shape
-    ff = weights.shape[1] // 2
+    ff = weights.shape[2]
     return pl.pallas_call(
         act_kernel,
         grid=(ff // CHUNK,),
         in_specs=[
             pl.BlockSpec((rows, width), lambda k: (0, 0)),
-            pl.BlockSpec((width, CHUNK), lambda k: (0, k)),
+            pl.BlockSpec((None, width, CHUNK), lambda k: (0, 0, k)),
         ],
         out_specs=pl.BlockSpec((rows, CHUNK), lambda k: (0, k)),
         out_shape=jax.ShapeDtypeStruct((rows, ff), jnp.bfloat16),
@@ -69,7 +69,7 @@
 
 def fused_back(normed, grad_in, standardized, inverse_deviation, gain_row, weights):
     rows, width = normed.shape
-    steps = weights.shape[1] // 2 // CHUNK
+    steps = weights.shape[2] // CHUNK
     whole = lambda k: (0, 0)
     return pl.pallas_call(
         fused_kernel,
@@ -80,8 +80,8 @@
             pl.BlockSpec((rows, width), whole),
             pl.BlockSpec(inverse_deviation.shape, whole),
             pl.BlockSpec((1, width), whole),
-            pl.BlockSpec((width, CHUNK), lambda k: (0, k)),
-            pl.BlockSpec((width, CHUNK), lambda k: (0, k + steps)),
+            pl.BlockSpec((None, width, CHUNK), lambda k: (0, 0, k)),
+            pl.BlockSpec((None, width, CHUNK), lambda k: (1, 0, k)),
         ],
         out_specs=[pl.BlockSpec((rows, width), whole), pl.BlockSpec((1, width), whole)],
         out_shape=[
@@ -90,8 +90,8 @@
         ],
         scratch_shapes=[pltpu.VMEM((rows, width), jnp.float32)],
         cost_estimate=pl.CostEstimate(
-            flops=6 * rows * width * weights.shape[1] // 2,
-            transcendentals=rows * weights.shape[1] // 2,
+            flops=6 * rows * width * weights.shape[2],
+            transcendentals=rows * weights.shape[2],
             bytes_accessed=2 * weights.size + 12 * rows * width,
         ),
     )(normed, grad_in, standardized, inverse_deviation, gain_row, weights, weights)
@@ -117,7 +117,7 @@
 
 def segment_back(grad_in, slope, standardized, inverse_deviation, gain_row, weights):
     rows, width = grad_in.shape
-    steps = weights.shape[1] // 2 // CHUNK
+    steps = weights.shape[2] // CHUNK
     whole = lambda k: (0, 0)
     return pl.pallas_call(
         segment_kernel,
@@ -128,8 +128,8 @@
             pl.BlockSpec((rows, width), whole),
             pl.BlockSpec(inverse_deviation.shape, whole),
             pl.BlockSpec((1, width), whole),
-            pl.BlockSpec((width, CHUNK), lambda k: (0, k)),
-            pl.BlockSpec((width, CHUNK), lambda k: (0, k + steps)),
+            pl.BlockSpec((None, width, CHUNK), lambda k: (0, 0, k)),
+            pl.BlockSpec((None, width, CHUNK), lambda k: (1, 0, k)),
         ],
         out_specs=[pl.BlockSpec((rows, width), whole), pl.BlockSpec((1, width), whole)],
         out_shape=[
@@ -138,7 +138,7 @@
         ],
         scratch_shapes=[pltpu.VMEM((rows, width), jnp.float32)],
         cost_estimate=pl.CostEstimate(
-            flops=4 * rows * width * weights.shape[1] // 2,
+            flops=4 * rows * width * weights.shape[2],
             transcendentals=0,
             bytes_accessed=2 * weights.size + 2 * rows * weights.shape[1] + 12 * rows * width,
         ),
@@ -165,8 +165,8 @@
     standardized_input = centered_input * inverse_deviation
     gain_vector = gains[0]
     normalized_input = (standardized_input * gain_vector).astype(jnp.bfloat16)
-    local = jnp.concatenate([w_in[0], w_out[0].T], axis=1)
-    weights = lax.all_gather(local, DP, axis=0, tiled=True)
+    local = jnp.stack([w_in[0], w_out[0].T])
+    weights = lax.all_gather(local, DP, axis=1, tiled=True)
 
     inverse_rows = jnp.broadcast_to(inverse_deviation, (rows, 128))
     gain_row = gain_vector[None, :]
@@ -175,7 +175,7 @@
     first = segments - 1
     slope = lax.cond(
         my_segment == first,
-        lambda: jnp.zeros((rows, weights.shape[1] // 2), jnp.bfloat16),
+        lambda: jnp.zeros((rows, weights.shape[2]), jnp.bfloat16),
         lambda: hidden_slope(normalized_input, weights),
     )
 

time: 227 us -> 227 us (level)
  no operation moved by 1% of the time
where the time goes in v8:
time: 227 us; the launch traced here: 226 us
  waiting for transfers between devices  157 us (69%)
  blocking collectives  28.4 us (13%)
  Pallas kernels  15.3 us (7%)
  between operations  14.2 us (6%)
  other arithmetic  7.36 us (3%)
  starting transfers between devices  2.7 us (1%)
    all_gather x1, waiting for transfers between devices, on_device(): weights = lax.all_gather(local, DP, axis=1, tiled=True)  102 us
    ppermute x3, waiting for transfers between devices, on_device(): current = lax.ppermute(result, 'segment', [(level, level - 1)])  55.3 us
    psum x3, blocking collectives, on_device(): gain_total = lax.psum(lax.psum(lax.psum(gain_local, 'core'), 'y'), 'z')  28.4 us
    pallas_call x1, Pallas kernels, segment_back(): pl.pallas_call(segment_kernel, grid=(steps,), in_specs=[pl.BlockSpec((row...  9.97 us
    pallas_call x1, Pallas kernels, hidden_slope(): pl.pallas_call(act_kernel, grid=(ff // CHUNK,), in_specs=[pl.BlockSpec((r...  5.3 us
  transfers between devices with their start and end apart: 4, of which 2 were waited for; matrix products, arithmetic and copies ran while one was open for 3% of the time, Pallas kernels for 2%

profile of v8, /device:TPU:8, one launch (start us, length us, event | category | flops | bytes accessed | tf_op | source)
XLA Modules:
  0.0 226.3 jit_solution(11337879178276063999)
XLA Ops:
  7.2 0.0 all-gather.2.cloned.1.call-start
  7.2 1.7 pad_maximum_fusion
  8.9 0.0 all-gather.2.cloned.1.call-update
  9.0 0.7 copy.10
  9.7 0.1 reduce-window.8
  9.8 0.1 reduce.1
  9.9 0.7 reduce.2
  10.7 0.1 convert_reduce_fusion.1
  10.8 0.7 select_reduce_fusion
  11.5 1.1 convert_reduce_fusion
  12.6 1.2 fusion.3
  13.9 1.5 fusion.1
  15.4 102.1 %all-gather.2.cloned.1.call-done = bf16[2,1536,3072]{2,1,0:T(8,128)(2,1)} async-done(((bf16[2,24,3072]{2,1,0:T(8,128)(2,1)}), bf16[2,1536,3072]{2,1,0:T(8,128)(2,1)}) %all-gather.2.cloned.1.call-update) | async-done | bytes 18874384 | tf_op jit(solution)/shard_map/all_gather | solution.py:169
  117.5 0.1 broadcast_in_dim.9
  117.6 0.1 conditional.5
  117.7 0.0 copy-start.1
  117.7 0.7 collective-permute-start
  118.4 5.3 %conditional.6 = (bf16[128,3072]{1,0:T(8,128)(2,1)S(1)}) conditional(s32[]{:T(128)} %convert_element_type.45, (bf16[128,1536]{1,0:T(8,128)(2,1)S(1)}, bf16[2,1536,3072]{2,1,0:T(8,128)(2,1)}) %tuple.44, () %tuple.45), branch_computations={%region_7.8_spmd, %region_8.9_spmd} | conditional | flops 1207959552 | bytes 10616840 | solution.py:176
  118.4 5.3 %branch_0_fun.1 = bf16[128,3072]{1,0:T(8,128)(2,1)S(1)} custom-call(bf16[128,1536]{1,0:T(8,128)(2,1)S(1)} %get-tuple-element.81.z_ref, bf16[2,1536,3072]{2,1,0:T(8,128)(2,1)} %get-tuple-element.82.w1_ref), custom_call_target="tpu_custom_call" | custom-call | flops 1207959552 | bytes 10616832 | tf_op jit(solution)/shard_map/cond/branch_0_fun/pallas_call | solution.py:22
  123.7 0.0 collective-permute-done
  123.7 0.0 copy-done.1
  123.7 0.7 collective-permute-start.1
  124.4 0.0 collective-permute-done.1
  124.5 0.0 copy-start
  124.5 1.3 collective-permute-start.2
  125.8 55.3 %collective-permute-done.2 = bf16[128,1536]{1,0:T(8,128)(2,1)S(1)} collective-permute-done((bf16[128,1536]{1,0:T(8,128)(2,1)S(1)}, bf16[128,1536]{1,0:T(8,128)(2,1)S(1)}, u32[]{:S(2)}, u32[]{:S(2)}) %collective-permute-start.2) | collective-permute-done | bytes 393248 | tf_op jit(solution)/shard_map/ppermute | solution.py:202
  181.1 0.0 copy-done
  181.1 10.0 %conditional.9 = ((f32[1,1536]{1,0:T(1,128)S(1)}, bf16[128,1536]{1,0:T(8,128)(2,1)})) conditional(s32[]{:T(128)} %convert_element_type.42, (f32[1,1536]{1,0:T(1,128)S(1)}, bf16[128,1536]{1,0:T(8,128)(2,1)}) %tuple.78, (bf16[128,1536]{1,0:T(8,128)(2,1)S(1)}, bf16[128,3072]{1,0:T(8,128)(2,1)S(1)}, f32[128,1536]{1,0:T(8,128)S(1)}, ...), branch_computations={%region_13.14_spmd, %region_14.15_spmd} | conditional | flops 2415919104 | bytes 21626904 | solution.py:198
  181.1 10.0 %branch_1_fun.7 = (bf16[128,1536]{1,0:T(8,128)(2,1)}, f32[1,1536]{1,0:T(1,128)S(1)}) custom-call(bf16[128,1536]{1,0:T(8,128)(2,1)S(1)} %get-tuple-element.95.g_ref, bf16[128,3072]{1,0:T(8,128)(2,1)S(1)} %get-tuple-element.96.act_ref, f32[128,1536]{1,0:T(8,128)S(1)} %get-tuple-element.97.xh_ref, f32[128,128]{1,0:T(8,128)S(1)} %get-tuple-element.98.inv_ref, ...), custom_call_target="tpu_custom_call" | custom-call | flops 2415919104 | bytes 21626880 | tf_op jit(solution)/shard_map/cond/branch_1_fun/pallas_call | solution.py:122
  191.1 2.5 %psum.21 = f32[1,1536]{1,0:T(1,128)S(1)} all-reduce(f32[1,1536]{1,0:T(1,128)S(1)} %get-tuple-element.120), channel_id=1, replica_groups=mesh['segment'=4,'z'=8,'y'=4,'core'=2] {'core'}, use_global_device_ids=true, to_apply=%region_15.16 | all-reduce | flops 1536 | bytes 12288 | tf_op jit(solution)/shard_map/psum | solution.py:203
  193.5 9.7 %psum.22 = f32[1,1536]{1,0:T(1,128)S(1)} all-reduce(f32[1,1536]{1,0:T(1,128)S(1)} %psum.21), channel_id=1, replica_groups=mesh['segment'=4,'z'=8,'y'=4,'core'=2] {'y'}, use_global_device_ids=true, to_apply=%region_16.17 | all-reduce | flops 1536 | bytes 12288 | tf_op jit(solution)/shard_map/psum | solution.py:203
  203.2 16.3 %psum.23 = f32[1,1536]{1,0:T(1,128)} all-reduce(f32[1,1536]{1,0:T(1,128)S(1)} %psum.22), channel_id=1, replica_groups=mesh['segment'=4,'z'=8,'y'=4,'core'=2] {'z'}, use_global_device_ids=true, to_apply=%region_17.18 | all-reduce | flops 1536 | bytes 12288 | tf_op jit(solution)/shard_map/psum | solution.py:203
  (8 shorter events, 0.1 us)
Async XLA Ops:
  7.2 110.4 %all-gather.2.cloned.1.call-start = ((), (), s32[]{:S(2)}) async-start(), calls=%async_computation | async-start | bytes 19169280 | tf_op jit(solution)/shard_map/all_gather | solution.py:169
  117.7 6.1 %copy-start.1 = (f32[1,1536]{1,0:T(1,128)S(1)}, f32[1,1536]{1,0:T(1,128)}, u32[]{:S(2)}) copy-start(f32[1,1536]{1,0:T(1,128)} %param.17) | copy-start | bytes 18436
  117.7 6.0 %collective-permute-start = (bf16[128,1536]{1,0:T(8,128)(2,1)S(1)}, bf16[128,1536]{1,0:T(8,128)(2,1)S(1)}, u32[]{:S(2)}, u32[]{:S(2)}) collective-permute-start(bf16[128,1536]{1,0:T(8,128)(2,1)S(1)} %get-tuple-element.111), channel_id=1, source_target_pairs={{192,128},{193,129},{194,130},{195,131},{196,132},{197,133},{198,1... | collective-permute-start | bytes 1179656 | tf_op jit(solution)/shard_map/ppermute | solution.py:202
  123.7 0.7 collective-permute-start.1
  124.5 56.6 %copy-start = (bf16[128,1536]{1,0:T(8,128)(2,1)}, bf16[128,1536]{1,0:T(8,128)(2,1)S(1)}, u32[]{:S(2)}) copy-start(bf16[128,1536]{1,0:T(8,128)(2,1)S(1)} %get-tuple-element.114) | copy-start | bytes 1179652
  124.5 56.6 %collective-permute-start.2 = (bf16[128,1536]{1,0:T(8,128)(2,1)S(1)}, bf16[128,1536]{1,0:T(8,128)(2,1)S(1)}, u32[]{:S(2)}, u32[]{:S(2)}) collective-permute-start(bf16[128,1536]{1,0:T(8,128)(2,1)S(1)} %get-tuple-element.114), channel_id=1, source_target_pairs={{64,0},{65,1},{66,2},{67,3},{68,4},{69,5},{70,6},{71,7},{72,8},{73... | collective-permute-start | bytes 1179656 | tf_op jit(solution)/shard_map/ppermute | solution.py:202
Sparse Core Ops, SparseCore 0:
  11.2 106.2 all-gather.1

commit v9 on v6

--- a/solution.py
+++ b/solution.py
@@ -200,7 +200,8 @@
         )
         if level > 0:
             current = lax.ppermute(result, "segment", [(level, level - 1)])
-    gain_total = lax.psum(lax.psum(lax.psum(gain_local, "core"), "y"), "z")
+    dense = gain_local.reshape(width // 128, 128)
+    gain_total = lax.psum(lax.psum(lax.psum(dense, "core"), "y"), "z").reshape(1, width)
     return (result[None], gain_total)
 
 

time: 227 us -> 227 us (level)
  no operation moved by 1% of the time
where the time goes in v9:
time: 227 us; the launch traced here: 226 us
  waiting for transfers between devices  158 us (70%)
  blocking collectives  28.5 us (13%)
  Pallas kernels  15.3 us (7%)
  between operations  14.2 us (6%)
  other arithmetic  7.37 us (3%)
  starting transfers between devices  2.7 us (1%)
    all_gather x1, waiting for transfers between devices, on_device(): weights = lax.all_gather(local, DP, axis=0, tiled=True)  102 us
    ppermute x3, waiting for transfers between devices, on_device(): current = lax.ppermute(result, 'segment', [(level, level - 1)])  55.4 us
    psum x1, blocking collectives, on_device(): lax.psum(lax.psum(lax.psum(dense, 'core'), 'y'), 'z').reshape(1, width)  16.3 us
    pallas_call x1, Pallas kernels, segment_back(): pl.pallas_call(segment_kernel, grid=(steps,), in_specs=[pl.BlockSpec((row...  9.97 us
    psum x1, blocking collectives, on_device(): lax.psum(lax.psum(dense, 'core'), 'y')  9.61 us
    pallas_call x1, Pallas kernels, hidden_slope(): pl.pallas_call(act_kernel, grid=(ff // CHUNK,), in_specs=[pl.BlockSpec((r...  5.3 us
  transfers between devices with their start and end apart: 4, of which 2 were waited for; matrix products, arithmetic and copies ran while one was open for 3% of the time, Pallas kernels for 2%

profile of v9, /device:TPU:8, one launch (start us, length us, event | category | flops | bytes accessed | tf_op | source)
XLA Modules:
  0.0 226.5 jit_solution(9100309850684031932)
XLA Ops:
  7.2 0.0 all-gather.2.cloned.1.call-start
  7.2 1.7 pad_maximum_fusion
  8.9 0.0 all-gather.2.cloned.1.call-update
  9.0 0.7 copy.10
  9.7 0.1 reduce-window.8
  9.8 0.1 reduce.1
  9.9 0.7 reduce.2
  10.7 0.1 convert_reduce_fusion.1
  10.8 0.7 select_reduce_fusion
  11.5 1.1 convert_reduce_fusion
  12.6 1.2 fusion.3
  13.9 1.5 fusion.1
  15.4 102.1 %all-gather.2.cloned.1.call-done = bf16[1536,6144]{1,0:T(8,128)(2,1)} async-done(((bf16[24,6144]{1,0:T(8,128)(2,1)}), bf16[1536,6144]{1,0:T(8,128)(2,1)}) %all-gather.2.cloned.1.call-update) | async-done | bytes 18874384 | tf_op jit(solution)/shard_map/all_gather | solution.py:169
  117.5 0.1 broadcast_in_dim.9
  117.6 0.1 conditional.5
  117.6 0.0 copy-start.1
  117.7 0.7 collective-permute-start
  118.4 5.3 %conditional.6 = (bf16[128,3072]{1,0:T(8,128)(2,1)S(1)}) conditional(s32[]{:T(128)} %convert_element_type.45, (bf16[128,1536]{1,0:T(8,128)(2,1)S(1)}, bf16[1536,6144]{1,0:T(8,128)(2,1)}) %tuple.44, () %tuple.45), branch_computations={%region_7.8_spmd, %region_8.9_spmd} | conditional | flops 1207959552 | bytes 10616840 | solution.py:176
  118.4 5.3 %branch_0_fun.1 = bf16[128,3072]{1,0:T(8,128)(2,1)S(1)} custom-call(bf16[128,1536]{1,0:T(8,128)(2,1)S(1)} %get-tuple-element.81.z_ref, bf16[1536,6144]{1,0:T(8,128)(2,1)} %get-tuple-element.82.w1_ref), custom_call_target="tpu_custom_call" | custom-call | flops 1207959552 | bytes 10616832 | tf_op jit(solution)/shard_map/cond/branch_0_fun/pallas_call | solution.py:22
  123.7 0.0 collective-permute-done
  123.7 0.0 copy-done.1
  123.7 0.7 collective-permute-start.1
  124.4 0.0 collective-permute-done.1
  124.5 0.0 copy-start
  124.5 1.3 collective-permute-start.2
  125.8 55.4 %collective-permute-done.2 = bf16[128,1536]{1,0:T(8,128)(2,1)S(1)} collective-permute-done((bf16[128,1536]{1,0:T(8,128)(2,1)S(1)}, bf16[128,1536]{1,0:T(8,128)(2,1)S(1)}, u32[]{:S(2)}, u32[]{:S(2)}) %collective-permute-start.2) | collective-permute-done | bytes 393248 | tf_op jit(solution)/shard_map/ppermute | solution.py:202
  181.1 0.0 copy-done
  181.1 10.0 %conditional.9 = ((f32[1,1536]{1,0:T(1,128)S(1)}, bf16[128,1536]{1,0:T(8,128)(2,1)})) conditional(s32[]{:T(128)} %convert_element_type.42, (f32[1,1536]{1,0:T(1,128)S(1)}, bf16[128,1536]{1,0:T(8,128)(2,1)}) %tuple.78, (bf16[128,1536]{1,0:T(8,128)(2,1)S(1)}, bf16[128,3072]{1,0:T(8,128)(2,1)S(1)}, f32[128,1536]{1,0:T(8,128)S(1)}, ...), branch_computations={%region_13.14_spmd, %region_14.15_spmd} | conditional | flops 2415919104 | bytes 22806552 | solution.py:198
  181.1 10.0 %branch_1_fun.7 = (bf16[128,1536]{1,0:T(8,128)(2,1)}, f32[1,1536]{1,0:T(1,128)S(1)}) custom-call(bf16[128,1536]{1,0:T(8,128)(2,1)S(1)} %get-tuple-element.95.g_ref, bf16[128,3072]{1,0:T(8,128)(2,1)S(1)} %get-tuple-element.96.act_ref, f32[128,1536]{1,0:T(8,128)S(1)} %get-tuple-element.97.xh_ref, f32[128,128]{1,0:T(8,128)S(1)} %get-tuple-element.98.inv_ref, ...), custom_call_target="tpu_custom_call" | custom-call | flops 2415919104 | bytes 22806528 | tf_op jit(solution)/shard_map/cond/branch_1_fun/pallas_call | solution.py:122
  191.1 2.5 %psum.21 = f32[12,128]{1,0:T(8,128)S(1)} all-reduce(f32[12,128]{1,0:T(8,128)S(1)} %bitcast.28), channel_id=1, replica_groups=mesh['segment'=4,'z'=8,'y'=4,'core'=2] {'core'}, use_global_device_ids=true, to_apply=%region_15.16 | all-reduce | flops 1536 | bytes 12288 | tf_op jit(solution)/shard_map/psum | solution.py:204
  193.6 9.6 %psum.22 = f32[12,128]{1,0:T(8,128)S(1)} all-reduce(f32[12,128]{1,0:T(8,128)S(1)} %psum.21), channel_id=1, replica_groups=mesh['segment'=4,'z'=8,'y'=4,'core'=2] {'y'}, use_global_device_ids=true, to_apply=%region_16.17 | all-reduce | flops 1536 | bytes 12288 | tf_op jit(solution)/shard_map/psum | solution.py:204
  203.3 16.3 %psum.23 = f32[1,1536]{1,0:T(1,128)} all-reduce(f32[1,1536]{1,0:T(1,128)S(1)} %bitcast.29), channel_id=1, replica_groups=mesh['segment'=4,'z'=8,'y'=4,'core'=2] {'z'}, use_global_device_ids=true, to_apply=%region_17.18 | all-reduce | flops 1536 | bytes 12288 | tf_op jit(solution)/shard_map/psum | solution.py:204
  (10 shorter events, 0.1 us)
Async XLA Ops:
  7.2 110.3 %all-gather.2.cloned.1.call-start = ((), (), s32[]{:S(2)}) async-start(), calls=%async_computation | async-start | bytes 19169280 | tf_op jit(solution)/shard_map/all_gather | solution.py:169
  117.6 6.1 %copy-start.1 = (f32[1,1536]{1,0:T(1,128)S(1)}, f32[1,1536]{1,0:T(1,128)}, u32[]{:S(2)}) copy-start(f32[1,1536]{1,0:T(1,128)} %param.17) | copy-start | bytes 18436
  117.7 6.0 %collective-permute-start = (bf16[128,1536]{1,0:T(8,128)(2,1)S(1)}, bf16[128,1536]{1,0:T(8,128)(2,1)S(1)}, u32[]{:S(2)}, u32[]{:S(2)}) collective-permute-start(bf16[128,1536]{1,0:T(8,128)(2,1)S(1)} %get-tuple-element.111), channel_id=1, source_target_pairs={{192,128},{193,129},{194,130},{195,131},{196,132},{197,133},{198,1... | collective-permute-start | bytes 1179656 | tf_op jit(solution)/shard_map/ppermute | solution.py:202
  123.7 0.7 collective-permute-start.1
  124.5 56.7 %copy-start = (bf16[128,1536]{1,0:T(8,128)(2,1)}, bf16[128,1536]{1,0:T(8,128)(2,1)S(1)}, u32[]{:S(2)}) copy-start(bf16[128,1536]{1,0:T(8,128)(2,1)S(1)} %get-tuple-element.114) | copy-start | bytes 1179652
  124.5 56.7 %collective-permute-start.2 = (bf16[128,1536]{1,0:T(8,128)(2,1)S(1)}, bf16[128,1536]{1,0:T(8,128)(2,1)S(1)}, u32[]{:S(2)}, u32[]{:S(2)}) collective-permute-start(bf16[128,1536]{1,0:T(8,128)(2,1)S(1)} %get-tuple-element.114), channel_id=1, source_target_pairs={{64,0},{65,1},{66,2},{67,3},{68,4},{69,5},{70,6},{71,7},{72,8},{73... | collective-permute-start | bytes 1179656 | tf_op jit(solution)/shard_map/ppermute | solution.py:202
Sparse Core Ops, SparseCore 0:
  11.3 106.1 all-gather.1

commit v10 on v6

--- a/solution.py
+++ b/solution.py
@@ -199,7 +199,14 @@
             my_segment == level, mine, keep, current, result, gain_local
         )
         if level > 0:
-            current = lax.ppermute(result, "segment", [(level, level - 1)])
+            half = rows // 2
+            pair = [(level, level - 1)]
+            current = jnp.concatenate(
+                [
+                    lax.ppermute(result[:half], "segment", pair),
+                    lax.ppermute(result[half:], "segment", pair),
+                ]
+            )
     gain_total = lax.psum(lax.psum(lax.psum(gain_local, "core"), "y"), "z")
     return (result[None], gain_total)
 

time: 227 us -> 228 us (level)
  starting transfers between devices: 2.7 us -> 5.32 us
    ppermute x3 -> x6, starting transfers between devices: 2.66 us -> 5.28 us  [the longest x3 2.64 us: on_device(): lax.ppermute(result[:half], 'segment', pair)]
    ppermute x3 -> x6, waiting for transfers between devices: 55.4 us -> 53.6 us  [the longest x3 51 us: on_device(): lax.ppermute(result[:half], 'segment', pair)]
  transfers between devices with their start and end apart: 4 -> 7, of which waited for: 2 -> 3; matrix products, arithmetic and copies ran while one was open for 3% -> 3% of each run, Pallas kernels for 2% -> 2%
where the time goes in v10:
time: 228 us
  waiting for transfers between devices  156 us (68%)
  blocking collectives  28.4 us (12%)
  Pallas kernels  15.3 us (7%)
  between operations  14.3 us (6%)
  other arithmetic  7.43 us (3%)
  starting transfers between devices  5.32 us (2%)
    all_gather x1, waiting for transfers between devices, on_device(): weights = lax.all_gather(local, DP, axis=0, tiled=True)  102 us
    ppermute x3, waiting for transfers between devices, on_device(): lax.ppermute(result[:half], 'segment', pair)  51 us
    psum x3, blocking collectives, on_device(): gain_total = lax.psum(lax.psum(lax.psum(gain_local, 'core'), 'y'), 'z')  28.4 us
    pallas_call x1, Pallas kernels, segment_back(): pl.pallas_call(segment_kernel, grid=(steps,), in_specs=[pl.BlockSpec((row...  9.99 us
    pallas_call x1, Pallas kernels, hidden_slope(): pl.pallas_call(act_kernel, grid=(ff // CHUNK,), in_specs=[pl.BlockSpec((r...  5.3 us
  transfers between devices with their start and end apart: 7, of which 3 were waited for; matrix products, arithmetic and copies ran while one was open for 3% of the time, Pallas kernels for 2%

profile of v10, /device:TPU:8, one launch (start us, length us, event | category | flops | bytes accessed | tf_op | source)
XLA Modules:
  0.0 227.5 jit_solution(18095913197038808555)
XLA Ops:
  7.2 0.0 all-gather.2.cloned.1.call-start
  7.2 1.7 pad_maximum_fusion.3
  8.9 0.0 all-gather.2.cloned.1.call-update
  9.0 0.7 copy.10
  9.7 0.1 reduce-window.8
  9.8 0.1 reduce.1
  9.9 0.7 reduce.2
  10.7 0.1 convert_reduce_fusion.1
  10.8 0.7 select_reduce_fusion
  11.5 1.1 convert_reduce_fusion
  12.6 1.2 fusion.3
  13.9 1.5 fusion.1
  15.4 102.1 %all-gather.2.cloned.1.call-done = bf16[1536,6144]{1,0:T(8,128)(2,1)} async-done(((bf16[24,6144]{1,0:T(8,128)(2,1)}), bf16[1536,6144]{1,0:T(8,128)(2,1)}) %all-gather.2.cloned.1.call-update) | async-done | bytes 18874384 | tf_op jit(solution)/shard_map/all_gather | solution.py:169
  117.5 0.1 broadcast_in_dim.9
  117.6 0.0 copy-start.1
  117.7 0.7 collective-permute-start
  118.3 0.7 collective-permute-start.1
  119.0 5.3 %conditional.6 = (bf16[128,3072]{1,0:T(8,128)(2,1)S(1)}) conditional(s32[]{:T(128)} %convert_element_type.45, (bf16[128,1536]{1,0:T(8,128)(2,1)S(1)}, bf16[1536,6144]{1,0:T(8,128)(2,1)}) %tuple.44, () %tuple.45), branch_computations={%region_7.8_spmd, %region_8.9_spmd} | conditional | flops 1207959552 | bytes 10616840 | solution.py:176
  119.0 5.3 %branch_0_fun.1 = bf16[128,3072]{1,0:T(8,128)(2,1)S(1)} custom-call(bf16[128,1536]{1,0:T(8,128)(2,1)S(1)} %get-tuple-element.81.z_ref, bf16[1536,6144]{1,0:T(8,128)(2,1)} %get-tuple-element.82.w1_ref), custom_call_target="tpu_custom_call" | custom-call | flops 1207959552 | bytes 10616832 | tf_op jit(solution)/shard_map/cond/branch_0_fun/pallas_call | solution.py:22
  124.4 0.0 collective-permute-done
  124.4 0.0 collective-permute-done.1
  124.4 0.0 copy-done.1
  124.5 0.7 collective-permute-start.2
  125.2 0.7 collective-permute-start.3
  125.8 0.0 collective-permute-done.2
  125.9 0.0 collective-permute-done.3
  125.9 0.0 copy-start
  126.0 1.3 collective-permute-start.4
  127.3 1.3 collective-permute-start.5
  128.6 51.0 %collective-permute-done.4 = bf16[64,1536]{1,0:T(8,128)(2,1)S(1)} collective-permute-done((bf16[64,1536]{1,0:T(8,128)(2,1)S(1)}, bf16[64,1536]{1,0:T(8,128)(2,1)S(1)}, u32[]{:S(2)}, u32[]{:S(2)}) %collective-permute-start.4) | collective-permute-done | bytes 196640 | tf_op jit(solution)/shard_map/ppermute | solution.py:206
  179.6 2.6 %collective-permute-done.5 = bf16[64,1536]{1,0:T(8,128)(2,1)S(1)} collective-permute-done((bf16[64,1536]{1,0:T(8,128)(2,1)S(1)}, bf16[64,1536]{1,0:T(8,128)(2,1)S(1)}, u32[]{:S(2)}, u32[]{:S(2)}) %collective-permute-start.5) | collective-permute-done | bytes 196640 | tf_op jit(solution)/shard_map/ppermute | solution.py:207
  182.2 0.0 copy-done
  182.2 10.0 %conditional.9 = ((f32[1,1536]{1,0:T(1,128)S(1)}, bf16[128,1536]{1,0:T(8,128)(2,1)})) conditional(s32[]{:T(128)} %convert_element_type.42, (f32[1,1536]{1,0:T(1,128)S(1)}, bf16[128,1536]{1,0:T(8,128)(2,1)}) %tuple.81, (bf16[128,1536]{1,0:T(8,128)(2,1)S(1)}, bf16[128,3072]{1,0:T(8,128)(2,1)S(1)}, f32[128,1536]{1,0:T(8,128)S(1)}, ...), branch_computations={%region_13.14_spmd, %region_14.15_spmd} | conditional | flops 2415919104 | bytes 22806552 | solution.py:198
  182.2 10.0 %branch_1_fun.7 = (bf16[128,1536]{1,0:T(8,128)(2,1)}, f32[1,1536]{1,0:T(1,128)S(1)}) custom-call(bf16[128,1536]{1,0:T(8,128)(2,1)S(1)} %get-tuple-element.95.g_ref, bf16[128,3072]{1,0:T(8,128)(2,1)S(1)} %get-tuple-element.96.act_ref, f32[128,1536]{1,0:T(8,128)S(1)} %get-tuple-element.97.xh_ref, f32[128,128]{1,0:T(8,128)S(1)} %get-tuple-element.98.inv_ref, ...), custom_call_target="tpu_custom_call" | custom-call | flops 2415919104 | bytes 22806528 | tf_op jit(solution)/shard_map/cond/branch_1_fun/pallas_call | solution.py:122
  192.2 2.5 %psum.21 = f32[1,1536]{1,0:T(1,128)S(1)} all-reduce(f32[1,1536]{1,0:T(1,128)S(1)} %get-tuple-element.120), channel_id=1, replica_groups=mesh['segment'=4,'z'=8,'y'=4,'core'=2] {'core'}, use_global_device_ids=true, to_apply=%region_15.16 | all-reduce | flops 1536 | bytes 12288 | tf_op jit(solution)/shard_map/psum | solution.py:210
  194.7 9.6 %psum.22 = f32[1,1536]{1,0:T(1,128)S(1)} all-reduce(f32[1,1536]{1,0:T(1,128)S(1)} %psum.21), channel_id=1, replica_groups=mesh['segment'=4,'z'=8,'y'=4,'core'=2] {'y'}, use_global_device_ids=true, to_apply=%region_16.17 | all-reduce | flops 1536 | bytes 12288 | tf_op jit(solution)/shard_map/psum | solution.py:210
  204.3 16.4 %psum.23 = f32[1,1536]{1,0:T(1,128)} all-reduce(f32[1,1536]{1,0:T(1,128)S(1)} %psum.22), channel_id=1, replica_groups=mesh['segment'=4,'z'=8,'y'=4,'core'=2] {'z'}, use_global_device_ids=true, to_apply=%region_17.18 | all-reduce | flops 1536 | bytes 12288 | tf_op jit(solution)/shard_map/psum | solution.py:210
  (14 shorter events, 0.2 us)
Async XLA Ops:
  7.2 110.3 %all-gather.2.cloned.1.call-start = ((), (), s32[]{:S(2)}) async-start(), calls=%async_computation | async-start | bytes 19169280 | tf_op jit(solution)/shard_map/all_gather | solution.py:169
  117.6 6.8 %copy-start.1 = (f32[1,1536]{1,0:T(1,128)S(1)}, f32[1,1536]{1,0:T(1,128)}, u32[]{:S(2)}) copy-start(f32[1,1536]{1,0:T(1,128)} %param.17) | copy-start | bytes 18436
  117.7 6.7 %collective-permute-start = (bf16[64,1536]{1,0:T(8,128)(2,1)S(1)}, bf16[64,1536]{1,0:T(8,128)(2,1)S(1)}, u32[]{:S(2)}, u32[]{:S(2)}) collective-permute-start(bf16[64,1536]{1,0:T(8,128)(2,1)S(1)} %get-tuple-element.128), channel_id=1, source_target_pairs={{192,128},{193,129},{194,130},{195,131},{196,132},{197,133},{198,1... | collective-permute-start | bytes 589832 | tf_op jit(solution)/shard_map/ppermute | solution.py:206
  118.3 6.0 %collective-permute-start.1 = (bf16[64,1536]{1,0:T(8,128)(2,1)S(1)}, bf16[64,1536]{1,0:T(8,128)(2,1)S(1)}, u32[]{:S(2)}, u32[]{:S(2)}) collective-permute-start(bf16[64,1536]{1,0:T(8,128)(2,1)S(1)} %get-tuple-element.129), channel_id=1, source_target_pairs={{192,128},{193,129},{194,130},{195,131},{196,132},{197,133},{198,1... | collective-permute-start | bytes 589832 | tf_op jit(solution)/shard_map/ppermute | solution.py:207
  124.5 1.4 collective-permute-start.2
  125.2 0.7 collective-permute-start.3
  125.9 56.3 %copy-start = (bf16[128,1536]{1,0:T(8,128)(2,1)}, bf16[128,1536]{1,0:T(8,128)(2,1)S(1)}, u32[]{:S(2)}) copy-start(bf16[128,1536]{1,0:T(8,128)(2,1)S(1)} %get-tuple-element.114) | copy-start | bytes 1179652
  126.0 53.6 %collective-permute-start.4 = (bf16[64,1536]{1,0:T(8,128)(2,1)S(1)}, bf16[64,1536]{1,0:T(8,128)(2,1)S(1)}, u32[]{:S(2)}, u32[]{:S(2)}) collective-permute-start(bf16[64,1536]{1,0:T(8,128)(2,1)S(1)} %get-tuple-element.124), channel_id=1, source_target_pairs={{64,0},{65,1},{66,2},{67,3},{68,4},{69,5},{70,6},{71,7},{72,8},{73... | collective-permute-start | bytes 589832 | tf_op jit(solution)/shard_map/ppermute | solution.py:206
  127.3 54.9 %collective-permute-start.5 = (bf16[64,1536]{1,0:T(8,128)(2,1)S(1)}, bf16[64,1536]{1,0:T(8,128)(2,1)S(1)}, u32[]{:S(2)}, u32[]{:S(2)}) collective-permute-start(bf16[64,1536]{1,0:T(8,128)(2,1)S(1)} %get-tuple-element.125), channel_id=1, source_target_pairs={{64,0},{65,1},{66,2},{67,3},{68,4},{69,5},{70,6},{71,7},{72,8},{73... | collective-permute-start | bytes 589832 | tf_op jit(solution)/shard_map/ppermute | solution.py:207
Sparse Core Ops, SparseCore 0:
  11.3 106.1 all-gather.1

commit v11 on v6

--- a/solution.py
+++ b/solution.py
@@ -200,7 +200,8 @@
         )
         if level > 0:
             current = lax.ppermute(result, "segment", [(level, level - 1)])
-    gain_total = lax.psum(lax.psum(lax.psum(gain_local, "core"), "y"), "z")
+    pair_sum = gain_local + lax.ppermute(gain_local, "core", [(0, 1), (1, 0)])
+    gain_total = lax.psum(lax.psum(pair_sum, "y"), "z")
     return (result[None], gain_total)
 
 

time: 227 us -> 226 us (level)
  blocking collectives: 28.4 us -> 26 us
    psum x3 -> x2, blocking collectives: 28.4 us -> 26 us  [on_device(): gain_total = lax.psum(lax.psum(pair_sum, 'y'), 'z')]
  transfers between devices with their start and end apart: 4 -> 5, of which waited for: 2 -> 3; matrix products, arithmetic and copies ran while one was open for 3% -> 3% of each run, Pallas kernels for 2% -> 2%
where the time goes in v11:
time: 226 us; the launch traced here: 225 us
  waiting for transfers between devices  159 us (70%)
  blocking collectives  26 us (12%)
  Pallas kernels  15.3 us (7%)
  between operations  14.2 us (6%)
  other arithmetic  7.36 us (3%)
  starting transfers between devices  2.7 us (1%)
    all_gather x1, waiting for transfers between devices, on_device(): weights = lax.all_gather(local, DP, axis=0, tiled=True)  102 us
    ppermute x3, waiting for transfers between devices, on_device(): current = lax.ppermute(result, 'segment', [(level, level - 1)])  55.4 us
    psum x2, blocking collectives, on_device(): gain_total = lax.psum(lax.psum(pair_sum, 'y'), 'z')  26 us
    pallas_call x1, Pallas kernels, segment_back(): pl.pallas_call(segment_kernel, grid=(steps,), in_specs=[pl.BlockSpec((row...  9.97 us
    pallas_call x1, Pallas kernels, hidden_slope(): pl.pallas_call(act_kernel, grid=(ff // CHUNK,), in_specs=[pl.BlockSpec((r...  5.3 us
  transfers between devices with their start and end apart: 5, of which 3 were waited for; matrix products, arithmetic and copies ran while one was open for 3% of the time, Pallas kernels for 2%

profile of v11, /device:TPU:8, one launch (start us, length us, event | category | flops | bytes accessed | tf_op | source)
XLA Modules:
  0.0 225.1 jit_solution(10246562556337562755)
XLA Ops:
  7.2 0.0 all-gather.2.cloned.1.call-start
  7.2 1.7 pad_maximum_fusion
  8.9 0.0 all-gather.2.cloned.1.call-update
  9.0 0.7 copy.10
  9.7 0.1 reduce-window.8
  9.8 0.1 reduce.1
  9.9 0.7 reduce.2
  10.7 0.1 convert_reduce_fusion.1
  10.8 0.7 select_reduce_fusion
  11.5 1.1 convert_reduce_fusion
  12.6 1.2 fusion.3
  13.9 1.5 fusion.1
  15.4 102.1 %all-gather.2.cloned.1.call-done = bf16[1536,6144]{1,0:T(8,128)(2,1)} async-done(((bf16[24,6144]{1,0:T(8,128)(2,1)}), bf16[1536,6144]{1,0:T(8,128)(2,1)}) %all-gather.2.cloned.1.call-update) | async-done | bytes 18874384 | tf_op jit(solution)/shard_map/all_gather | solution.py:169
  117.5 0.1 broadcast_in_dim.9
  117.6 0.1 conditional.5
  117.6 0.0 copy-start.1
  117.7 0.7 collective-permute-start
  118.4 5.3 %conditional.6 = (bf16[128,3072]{1,0:T(8,128)(2,1)S(1)}) conditional(s32[]{:T(128)} %convert_element_type.45, (bf16[128,1536]{1,0:T(8,128)(2,1)S(1)}, bf16[1536,6144]{1,0:T(8,128)(2,1)}) %tuple.44, () %tuple.45), branch_computations={%region_7.8_spmd, %region_8.9_spmd} | conditional | flops 1207959552 | bytes 10616840 | solution.py:176
  118.4 5.3 %branch_0_fun.1 = bf16[128,3072]{1,0:T(8,128)(2,1)S(1)} custom-call(bf16[128,1536]{1,0:T(8,128)(2,1)S(1)} %get-tuple-element.81.z_ref, bf16[1536,6144]{1,0:T(8,128)(2,1)} %get-tuple-element.82.w1_ref), custom_call_target="tpu_custom_call" | custom-call | flops 1207959552 | bytes 10616832 | tf_op jit(solution)/shard_map/cond/branch_0_fun/pallas_call | solution.py:22
  123.7 0.0 collective-permute-done
  123.7 0.0 copy-done.1
  123.7 0.7 collective-permute-start.1
  124.4 0.0 collective-permute-done.1
  124.5 0.0 copy-start
  124.5 1.3 collective-permute-start.2
  125.8 55.4 %collective-permute-done.2 = bf16[128,1536]{1,0:T(8,128)(2,1)S(1)} collective-permute-done((bf16[128,1536]{1,0:T(8,128)(2,1)S(1)}, bf16[128,1536]{1,0:T(8,128)(2,1)S(1)}, u32[]{:S(2)}, u32[]{:S(2)}) %collective-permute-start.2) | collective-permute-done | bytes 393248 | tf_op jit(solution)/shard_map/ppermute | solution.py:202
  181.1 0.0 copy-done
  181.1 10.0 %conditional.9 = ((f32[1,1536]{1,0:T(1,128)S(1)}, bf16[128,1536]{1,0:T(8,128)(2,1)})) conditional(s32[]{:T(128)} %convert_element_type.42, (f32[1,1536]{1,0:T(1,128)S(1)}, bf16[128,1536]{1,0:T(8,128)(2,1)}) %tuple.78, (bf16[128,1536]{1,0:T(8,128)(2,1)S(1)}, bf16[128,3072]{1,0:T(8,128)(2,1)S(1)}, f32[128,1536]{1,0:T(8,128)S(1)}, ...), branch_computations={%region_13.14_spmd, %region_14.15_spmd} | conditional | flops 2415919104 | bytes 22806552 | solution.py:198
  181.1 10.0 %branch_1_fun.7 = (bf16[128,1536]{1,0:T(8,128)(2,1)}, f32[1,1536]{1,0:T(1,128)S(1)}) custom-call(bf16[128,1536]{1,0:T(8,128)(2,1)S(1)} %get-tuple-element.95.g_ref, bf16[128,3072]{1,0:T(8,128)(2,1)S(1)} %get-tuple-element.96.act_ref, f32[128,1536]{1,0:T(8,128)S(1)} %get-tuple-element.97.xh_ref, f32[128,128]{1,0:T(8,128)S(1)} %get-tuple-element.98.inv_ref, ...), custom_call_target="tpu_custom_call" | custom-call | flops 2415919104 | bytes 22806528 | tf_op jit(solution)/shard_map/cond/branch_1_fun/pallas_call | solution.py:122
  191.1 0.0 collective-permute-start.3
  191.1 1.2 collective-permute-done.3
  192.3 9.6 %psum.14 = f32[1,1536]{1,0:T(1,128)S(1)} all-reduce(f32[1,1536]{1,0:T(1,128)S(1)} %add.52), channel_id=1, replica_groups=mesh['segment'=4,'z'=8,'y'=4,'core'=2] {'y'}, use_global_device_ids=true, to_apply=%region_15.16 | all-reduce | flops 1536 | bytes 12288 | tf_op jit(solution)/shard_map/psum | solution.py:204
  201.9 16.3 %psum.15 = f32[1,1536]{1,0:T(1,128)} all-reduce(f32[1,1536]{1,0:T(1,128)S(1)} %psum.14), channel_id=1, replica_groups=mesh['segment'=4,'z'=8,'y'=4,'core'=2] {'z'}, use_global_device_ids=true, to_apply=%region_16.17 | all-reduce | flops 1536 | bytes 12288 | tf_op jit(solution)/shard_map/psum | solution.py:204
  (9 shorter events, 0.1 us)
Async XLA Ops:
  7.2 110.3 %all-gather.2.cloned.1.call-start = ((), (), s32[]{:S(2)}) async-start(), calls=%async_computation | async-start | bytes 19169280 | tf_op jit(solution)/shard_map/all_gather | solution.py:169
  117.6 6.1 %copy-start.1 = (f32[1,1536]{1,0:T(1,128)S(1)}, f32[1,1536]{1,0:T(1,128)}, u32[]{:S(2)}) copy-start(f32[1,1536]{1,0:T(1,128)} %param.17) | copy-start | bytes 18436
  117.7 6.0 %collective-permute-start = (bf16[128,1536]{1,0:T(8,128)(2,1)S(1)}, bf16[128,1536]{1,0:T(8,128)(2,1)S(1)}, u32[]{:S(2)}, u32[]{:S(2)}) collective-permute-start(bf16[128,1536]{1,0:T(8,128)(2,1)S(1)} %get-tuple-element.111), channel_id=1, source_target_pairs={{192,128},{193,129},{194,130},{195,131},{196,132},{197,133},{198,1... | collective-permute-start | bytes 1179656 | tf_op jit(solution)/shard_map/ppermute | solution.py:202
  123.7 0.7 collective-permute-start.1
  124.5 56.7 %copy-start = (bf16[128,1536]{1,0:T(8,128)(2,1)}, bf16[128,1536]{1,0:T(8,128)(2,1)S(1)}, u32[]{:S(2)}) copy-start(bf16[128,1536]{1,0:T(8,128)(2,1)S(1)} %get-tuple-element.114) | copy-start | bytes 1179652
  124.5 56.7 %collective-permute-start.2 = (bf16[128,1536]{1,0:T(8,128)(2,1)S(1)}, bf16[128,1536]{1,0:T(8,128)(2,1)S(1)}, u32[]{:S(2)}, u32[]{:S(2)}) collective-permute-start(bf16[128,1536]{1,0:T(8,128)(2,1)S(1)} %get-tuple-element.114), channel_id=1, source_target_pairs={{64,0},{65,1},{66,2},{67,3},{68,4},{69,5},{70,6},{71,7},{72,8},{73... | collective-permute-start | bytes 1179656 | tf_op jit(solution)/shard_map/ppermute | solution.py:202
  191.1 1.2 collective-permute-start.3
Sparse Core Ops, SparseCore 0:
  11.3 106.1 all-gather.1

commit v12 on v11

--- a/solution.py
+++ b/solution.py
@@ -201,7 +201,9 @@
         if level > 0:
             current = lax.ppermute(result, "segment", [(level, level - 1)])
     pair_sum = gain_local + lax.ppermute(gain_local, "core", [(0, 1), (1, 0)])
-    gain_total = lax.psum(lax.psum(pair_sum, "y"), "z")
+    for step in (1, 2):
+        pair_sum = pair_sum + lax.ppermute(pair_sum, "y", [(i, i ^ step) for i in range(4)])
+    gain_total = lax.psum(pair_sum, "z")
     return (result[None], gain_total)
 
 

time: 226 us -> 225 us (level)
  blocking collectives: 26 us -> 16.4 us
  waiting for transfers between devices: 159 us -> 164 us
  starting transfers between devices: 2.7 us -> 6.2 us
    psum x2 -> x1, blocking collectives: 26 us -> 16.4 us  [on_device(): gain_total = lax.psum(pair_sum, 'z')]
    ppermute x0 -> x2, waiting for transfers between devices: none -> 5.44 us  [on_device(): lax.ppermute(pair_sum, 'y', [(i, i ^ step) for i in range(4)])]
    ppermute x0 -> x2, starting transfers between devices: none -> 3.5 us  [on_device(): lax.ppermute(pair_sum, 'y', [(i, i ^ step) for i in range(4)])]
  transfers between devices with their start and end apart: 5 -> 7, of which waited for: 3 -> 5; matrix products, arithmetic and copies ran while one was open for 3% -> 3% of each run, Pallas kernels for 2% -> 2%
where the time goes in v12:
time: 225 us; the launch traced here: 224 us
  waiting for transfers between devices  164 us (73%)
  blocking collectives  16.4 us (7%)
  Pallas kernels  15.3 us (7%)
  between operations  14.2 us (6%)
  other arithmetic  7.37 us (3%)
  starting transfers between devices  6.2 us (3%)
    all_gather x1, waiting for transfers between devices, on_device(): weights = lax.all_gather(local, DP, axis=0, tiled=True)  102 us
    ppermute x3, waiting for transfers between devices, on_device(): current = lax.ppermute(result, 'segment', [(level, level - 1)])  55.3 us
    psum x1, blocking collectives, on_device(): gain_total = lax.psum(pair_sum, 'z')  16.4 us
    pallas_call x1, Pallas kernels, segment_back(): pl.pallas_call(segment_kernel, grid=(steps,), in_specs=[pl.BlockSpec((row...  9.97 us
    ppermute x2, waiting for transfers between devices, on_device(): lax.ppermute(pair_sum, 'y', [(i, i ^ step) for i in range(4)])  5.44 us
    pallas_call x1, Pallas kernels, hidden_slope(): pl.pallas_call(act_kernel, grid=(ff // CHUNK,), in_specs=[pl.BlockSpec((r...  5.3 us
  transfers between devices with their start and end apart: 7, of which 5 were waited for; matrix products, arithmetic and copies ran while one was open for 3% of the time, Pallas kernels for 2%

profile of v12, /device:TPU:8, one launch (start us, length us, event | category | flops | bytes accessed | tf_op | source)
XLA Modules:
  0.0 224.4 jit_solution(17058480506635084232)
XLA Ops:
  7.2 0.0 all-gather.2.cloned.1.call-start
  7.2 1.7 pad_maximum_fusion
  8.9 0.0 all-gather.2.cloned.1.call-update
  9.0 0.7 copy.10
  9.7 0.1 reduce-window.8
  9.8 0.1 reduce.1
  9.9 0.7 reduce.2
  10.7 0.1 convert_reduce_fusion.1
  10.8 0.7 select_reduce_fusion
  11.5 1.1 convert_reduce_fusion
  12.6 1.2 fusion.3
  13.9 1.5 fusion.1
  15.4 102.1 %all-gather.2.cloned.1.call-done = bf16[1536,6144]{1,0:T(8,128)(2,1)} async-done(((bf16[24,6144]{1,0:T(8,128)(2,1)}), bf16[1536,6144]{1,0:T(8,128)(2,1)}) %all-gather.2.cloned.1.call-update) | async-done | bytes 18874384 | tf_op jit(solution)/shard_map/all_gather | solution.py:169
  117.5 0.1 broadcast_in_dim.9
  117.6 0.1 conditional.5
  117.6 0.0 copy-start.1
  117.7 0.7 collective-permute-start
  118.4 5.3 %conditional.6 = (bf16[128,3072]{1,0:T(8,128)(2,1)S(1)}) conditional(s32[]{:T(128)} %convert_element_type.45, (bf16[128,1536]{1,0:T(8,128)(2,1)S(1)}, bf16[1536,6144]{1,0:T(8,128)(2,1)}) %tuple.44, () %tuple.45), branch_computations={%region_7.8_spmd, %region_8.9_spmd} | conditional | flops 1207959552 | bytes 10616840 | solution.py:176
  118.4 5.3 %branch_0_fun.1 = bf16[128,3072]{1,0:T(8,128)(2,1)S(1)} custom-call(bf16[128,1536]{1,0:T(8,128)(2,1)S(1)} %get-tuple-element.81.z_ref, bf16[1536,6144]{1,0:T(8,128)(2,1)} %get-tuple-element.82.w1_ref), custom_call_target="tpu_custom_call" | custom-call | flops 1207959552 | bytes 10616832 | tf_op jit(solution)/shard_map/cond/branch_0_fun/pallas_call | solution.py:22
  123.7 0.0 collective-permute-done
  123.7 0.0 copy-done.1
  123.7 0.7 collective-permute-start.1
  124.4 0.0 collective-permute-done.1
  124.4 0.0 copy-start
  124.5 1.3 collective-permute-start.2
  125.8 55.3 %collective-permute-done.2 = bf16[128,1536]{1,0:T(8,128)(2,1)S(1)} collective-permute-done((bf16[128,1536]{1,0:T(8,128)(2,1)S(1)}, bf16[128,1536]{1,0:T(8,128)(2,1)S(1)}, u32[]{:S(2)}, u32[]{:S(2)}) %collective-permute-start.2) | collective-permute-done | bytes 393248 | tf_op jit(solution)/shard_map/ppermute | solution.py:202
  181.1 0.0 copy-done
  181.1 10.0 %conditional.9 = ((f32[1,1536]{1,0:T(1,128)S(1)}, bf16[128,1536]{1,0:T(8,128)(2,1)})) conditional(s32[]{:T(128)} %convert_element_type.42, (f32[1,1536]{1,0:T(1,128)S(1)}, bf16[128,1536]{1,0:T(8,128)(2,1)}) %tuple.78, (bf16[128,1536]{1,0:T(8,128)(2,1)S(1)}, bf16[128,3072]{1,0:T(8,128)(2,1)S(1)}, f32[128,1536]{1,0:T(8,128)S(1)}, ...), branch_computations={%region_13.14_spmd, %region_14.15_spmd} | conditional | flops 2415919104 | bytes 22806552 | solution.py:198
  181.1 10.0 %branch_1_fun.7 = (bf16[128,1536]{1,0:T(8,128)(2,1)}, f32[1,1536]{1,0:T(1,128)S(1)}) custom-call(bf16[128,1536]{1,0:T(8,128)(2,1)S(1)} %get-tuple-element.95.g_ref, bf16[128,3072]{1,0:T(8,128)(2,1)S(1)} %get-tuple-element.96.act_ref, f32[128,1536]{1,0:T(8,128)S(1)} %get-tuple-element.97.xh_ref, f32[128,128]{1,0:T(8,128)S(1)} %get-tuple-element.98.inv_ref, ...), custom_call_target="tpu_custom_call" | custom-call | flops 2415919104 | bytes 22806528 | tf_op jit(solution)/shard_map/cond/branch_1_fun/pallas_call | solution.py:122
  191.1 0.0 collective-permute-start.3
  191.1 1.2 collective-permute-done.3
  192.3 1.9 collective-permute-start.4
  194.2 1.8 collective-permute-done.4
  196.0 1.6 collective-permute-start.5
  197.5 3.7 %collective-permute-done.5 = f32[1,1536]{1,0:T(1,128)S(1)} collective-permute-done((f32[1,1536]{1,0:T(1,128)S(1)}, f32[1,1536]{1,0:T(1,128)S(1)}, u32[]{:S(2)}, u32[]{:S(2)}) %collective-permute-start.5) | collective-permute-done | bytes 6176 | tf_op jit(solution)/shard_map/ppermute | solution.py:205
  201.2 16.4 %psum.7 = f32[1,1536]{1,0:T(1,128)} all-reduce(f32[1,1536]{1,0:T(1,128)S(1)} %add.58), channel_id=1, replica_groups=mesh['segment'=4,'z'=8,'y'=4,'core'=2] {'z'}, use_global_device_ids=true, to_apply=%region_15.16 | all-reduce | flops 1536 | bytes 12288 | tf_op jit(solution)/shard_map/psum | solution.py:206
  (11 shorter events, 0.1 us)
Async XLA Ops:
  7.2 110.3 %all-gather.2.cloned.1.call-start = ((), (), s32[]{:S(2)}) async-start(), calls=%async_computation | async-start | bytes 19169280 | tf_op jit(solution)/shard_map/all_gather | solution.py:169
  117.6 6.1 %copy-start.1 = (f32[1,1536]{1,0:T(1,128)S(1)}, f32[1,1536]{1,0:T(1,128)}, u32[]{:S(2)}) copy-start(f32[1,1536]{1,0:T(1,128)} %param.17) | copy-start | bytes 18436
  117.7 6.0 %collective-permute-start = (bf16[128,1536]{1,0:T(8,128)(2,1)S(1)}, bf16[128,1536]{1,0:T(8,128)(2,1)S(1)}, u32[]{:S(2)}, u32[]{:S(2)}) collective-permute-start(bf16[128,1536]{1,0:T(8,128)(2,1)S(1)} %get-tuple-element.111), channel_id=1, source_target_pairs={{192,128},{193,129},{194,130},{195,131},{196,132},{197,133},{198,1... | collective-permute-start | bytes 1179656 | tf_op jit(solution)/shard_map/ppermute | solution.py:202
  123.7 0.7 collective-permute-start.1
  124.4 56.7 %copy-start = (bf16[128,1536]{1,0:T(8,128)(2,1)}, bf16[128,1536]{1,0:T(8,128)(2,1)S(1)}, u32[]{:S(2)}) copy-start(bf16[128,1536]{1,0:T(8,128)(2,1)S(1)} %get-tuple-element.114) | copy-start | bytes 1179652
  124.5 56.6 %collective-permute-start.2 = (bf16[128,1536]{1,0:T(8,128)(2,1)S(1)}, bf16[128,1536]{1,0:T(8,128)(2,1)S(1)}, u32[]{:S(2)}, u32[]{:S(2)}) collective-permute-start(bf16[128,1536]{1,0:T(8,128)(2,1)S(1)} %get-tuple-element.114), channel_id=1, source_target_pairs={{64,0},{65,1},{66,2},{67,3},{68,4},{69,5},{70,6},{71,7},{72,8},{73... | collective-permute-start | bytes 1179656 | tf_op jit(solution)/shard_map/ppermute | solution.py:202
  191.1 1.2 collective-permute-start.3
  192.3 3.7 %collective-permute-start.4 = (f32[1,1536]{1,0:T(1,128)S(1)}, f32[1,1536]{1,0:T(1,128)S(1)}, u32[]{:S(2)}, u32[]{:S(2)}) collective-permute-start(f32[1,1536]{1,0:T(1,128)S(1)} %add.56), channel_id=1, source_target_pairs={{0,2},{2,0},{4,6},{6,4},{1,3},{3,1},{5,7},{7,5},{8,10},{10,8},{12,... | collective-permute-start | bytes 18440 | tf_op jit(solution)/shard_map/ppermute | solution.py:205
  196.0 5.2 %collective-permute-start.5 = (f32[1,1536]{1,0:T(1,128)S(1)}, f32[1,1536]{1,0:T(1,128)S(1)}, u32[]{:S(2)}, u32[]{:S(2)}) collective-permute-start(f32[1,1536]{1,0:T(1,128)S(1)} %add.57), channel_id=1, source_target_pairs={{0,4},{2,6},{4,0},{6,2},{1,5},{3,7},{5,1},{7,3},{8,12},{10,14},{12... | collective-permute-start | bytes 18440 | tf_op jit(solution)/shard_map/ppermute | solution.py:205
Sparse Core Ops, SparseCore 0:
  11.3 106.1 all-gather.1

commit v13 on v12

--- a/solution.py
+++ b/solution.py
@@ -203,7 +203,9 @@
     pair_sum = gain_local + lax.ppermute(gain_local, "core", [(0, 1), (1, 0)])
     for step in (1, 2):
         pair_sum = pair_sum + lax.ppermute(pair_sum, "y", [(i, i ^ step) for i in range(4)])
-    gain_total = lax.psum(pair_sum, "z")
+    for step in (1, 2, 4):
+        pair_sum = pair_sum + lax.ppermute(pair_sum, "z", [(i, i ^ step) for i in range(8)])
+    gain_total = pair_sum
     return (result[None], gain_total)
 
 

time: 225 us -> 225 us (level)
  blocking collectives: 16.4 us -> 0 us
  waiting for transfers between devices: 164 us -> 175 us
  starting transfers between devices: 6.2 us -> 10.9 us
    psum x1 -> x0, blocking collectives: 16.4 us -> none  [on_device(): gain_total = lax.psum(pair_sum, 'z')]
    ppermute x0 -> x3, waiting for transfers between devices: none -> 11.2 us  [on_device(): lax.ppermute(pair_sum, 'z', [(i, i ^ step) for i in range(8)])]
    ppermute x0 -> x3, starting transfers between devices: none -> 4.73 us  [on_device(): lax.ppermute(pair_sum, 'z', [(i, i ^ step) for i in range(8)])]
  transfers between devices with their start and end apart: 7 -> 10, of which waited for: 5 -> 8; matrix products, arithmetic and copies ran while one was open for 3% -> 3% of each run, Pallas kernels for 2% -> 2%
where the time goes in v13:
time: 225 us
  waiting for transfers between devices  175 us (78%)
  Pallas kernels  15.3 us (7%)
  between operations  14.2 us (6%)
  starting transfers between devices  10.9 us (5%)
  other arithmetic  7.99 us (4%)
    all_gather x1, waiting for transfers between devices, on_device(): weights = lax.all_gather(local, DP, axis=0, tiled=True)  102 us
    ppermute x3, waiting for transfers between devices, on_device(): current = lax.ppermute(result, 'segment', [(level, level - 1)])  55.3 us
    ppermute x3, waiting for transfers between devices, on_device(): lax.ppermute(pair_sum, 'z', [(i, i ^ step) for i in range(8)])  11.2 us
    pallas_call x1, Pallas kernels, segment_back(): pl.pallas_call(segment_kernel, grid=(steps,), in_specs=[pl.BlockSpec((row...  9.97 us
    ppermute x2, waiting for transfers between devices, on_device(): lax.ppermute(pair_sum, 'y', [(i, i ^ step) for i in range(4)])  5.44 us
    pallas_call x1, Pallas kernels, hidden_slope(): pl.pallas_call(act_kernel, grid=(ff // CHUNK,), in_specs=[pl.BlockSpec((r...  5.3 us
    ppermute x3, starting transfers between devices, on_device(): lax.ppermute(pair_sum, 'z', [(i, i ^ step) for i in range(8)])  4.73 us
  transfers between devices with their start and end apart: 10, of which 8 were waited for; matrix products, arithmetic and copies ran while one was open for 3% of the time, Pallas kernels for 2%

profile of v13, /device:TPU:8, one launch (start us, length us, event | category | flops | bytes accessed | tf_op | source)
XLA Modules:
  0.0 224.7 jit_solution(11363228540954055846)
XLA Ops:
  7.2 0.0 all-gather.2.cloned.1.call-start
  7.2 1.7 pad_maximum_fusion
  8.9 0.0 all-gather.2.cloned.1.call-update
  9.0 0.7 copy.10
  9.7 0.1 reduce-window.8
  9.8 0.1 reduce.1
  9.9 0.7 reduce.2
  10.7 0.1 convert_reduce_fusion.1
  10.8 0.7 select_reduce_fusion
  11.5 1.1 convert_reduce_fusion
  12.6 1.2 fusion.3
  13.9 1.5 fusion.1
  15.4 102.1 %all-gather.2.cloned.1.call-done = bf16[1536,6144]{1,0:T(8,128)(2,1)} async-done(((bf16[24,6144]{1,0:T(8,128)(2,1)}), bf16[1536,6144]{1,0:T(8,128)(2,1)}) %all-gather.2.cloned.1.call-update) | async-done | bytes 18874384 | tf_op jit(solution)/shard_map/all_gather | solution.py:169
  117.5 0.1 broadcast_in_dim.9
  117.6 0.1 conditional.5
  117.6 0.0 copy-start.1
  117.7 0.7 collective-permute-start
  118.4 5.3 %conditional.6 = (bf16[128,3072]{1,0:T(8,128)(2,1)S(1)}) conditional(s32[]{:T(128)} %convert_element_type.45, (bf16[128,1536]{1,0:T(8,128)(2,1)S(1)}, bf16[1536,6144]{1,0:T(8,128)(2,1)}) %tuple.44, () %tuple.45), branch_computations={%region_7.8_spmd, %region_8.9_spmd} | conditional | flops 1207959552 | bytes 10616840 | solution.py:176
  118.4 5.3 %branch_0_fun.1 = bf16[128,3072]{1,0:T(8,128)(2,1)S(1)} custom-call(bf16[128,1536]{1,0:T(8,128)(2,1)S(1)} %get-tuple-element.81.z_ref, bf16[1536,6144]{1,0:T(8,128)(2,1)} %get-tuple-element.82.w1_ref), custom_call_target="tpu_custom_call" | custom-call | flops 1207959552 | bytes 10616832 | tf_op jit(solution)/shard_map/cond/branch_0_fun/pallas_call | solution.py:22
  123.7 0.0 collective-permute-done
  123.7 0.0 copy-done.1
  123.7 0.7 collective-permute-start.1
  124.4 0.0 collective-permute-done.1
  124.4 0.0 copy-start
  124.5 1.3 collective-permute-start.2
  125.8 55.3 %collective-permute-done.2 = bf16[128,1536]{1,0:T(8,128)(2,1)S(1)} collective-permute-done((bf16[128,1536]{1,0:T(8,128)(2,1)S(1)}, bf16[128,1536]{1,0:T(8,128)(2,1)S(1)}, u32[]{:S(2)}, u32[]{:S(2)}) %collective-permute-start.2) | collective-permute-done | bytes 393248 | tf_op jit(solution)/shard_map/ppermute | solution.py:202
  181.1 0.0 copy-done
  181.1 10.0 %conditional.9 = ((f32[1,1536]{1,0:T(1,128)S(1)}, bf16[128,1536]{1,0:T(8,128)(2,1)})) conditional(s32[]{:T(128)} %convert_element_type.42, (f32[1,1536]{1,0:T(1,128)S(1)}, bf16[128,1536]{1,0:T(8,128)(2,1)}) %tuple.78, (bf16[128,1536]{1,0:T(8,128)(2,1)S(1)}, bf16[128,3072]{1,0:T(8,128)(2,1)S(1)}, f32[128,1536]{1,0:T(8,128)S(1)}, ...), branch_computations={%region_13.14_spmd, %region_14.15_spmd} | conditional | flops 2415919104 | bytes 22806552 | solution.py:198
  181.1 10.0 %branch_1_fun.7 = (bf16[128,1536]{1,0:T(8,128)(2,1)}, f32[1,1536]{1,0:T(1,128)S(1)}) custom-call(bf16[128,1536]{1,0:T(8,128)(2,1)S(1)} %get-tuple-element.95.g_ref, bf16[128,3072]{1,0:T(8,128)(2,1)S(1)} %get-tuple-element.96.act_ref, f32[128,1536]{1,0:T(8,128)S(1)} %get-tuple-element.97.xh_ref, f32[128,128]{1,0:T(8,128)S(1)} %get-tuple-element.98.inv_ref, ...), custom_call_target="tpu_custom_call" | custom-call | flops 2415919104 | bytes 22806528 | tf_op jit(solution)/shard_map/cond/branch_1_fun/pallas_call | solution.py:122
  191.1 0.0 collective-permute-start.3
  191.1 1.2 collective-permute-done.3
  192.3 1.9 collective-permute-start.4
  194.2 1.8 collective-permute-done.4
  196.0 1.6 collective-permute-start.5
  197.5 3.7 %collective-permute-done.5 = f32[1,1536]{1,0:T(1,128)S(1)} collective-permute-done((f32[1,1536]{1,0:T(1,128)S(1)}, f32[1,1536]{1,0:T(1,128)S(1)}, u32[]{:S(2)}, u32[]{:S(2)}) %collective-permute-start.5) | collective-permute-done | bytes 6176 | tf_op jit(solution)/shard_map/ppermute | solution.py:205
  201.2 0.1 collective-permute-start.6
  201.3 3.6 %collective-permute-done.6 = f32[1,1536]{1,0:T(1,128)S(1)} collective-permute-done((f32[1,1536]{1,0:T(1,128)S(1)}, f32[1,1536]{1,0:T(1,128)S(1)}, u32[]{:S(2)}, u32[]{:S(2)}) %collective-permute-start.6) | collective-permute-done | bytes 6176 | tf_op jit(solution)/shard_map/ppermute | solution.py:207
  204.9 1.6 collective-permute-start.7
  206.5 3.1 %collective-permute-done.7 = f32[1,1536]{1,0:T(1,128)S(1)} collective-permute-done((f32[1,1536]{1,0:T(1,128)S(1)}, f32[1,1536]{1,0:T(1,128)S(1)}, u32[]{:S(2)}, u32[]{:S(2)}) %collective-permute-start.7) | collective-permute-done | bytes 6176 | tf_op jit(solution)/shard_map/ppermute | solution.py:207
  209.6 3.1 %collective-permute-start.8 = (f32[1,1536]{1,0:T(1,128)S(1)}, f32[1,1536]{1,0:T(1,128)S(1)}, u32[]{:S(2)}, u32[]{:S(2)}) collective-permute-start(f32[1,1536]{1,0:T(1,128)S(1)} %add.67), channel_id=1, source_target_pairs={{0,32},{8,40},{16,48},{24,56},{32,0},{40,8},{48,16},{56,24},{1,33}... | collective-permute-start | bytes 18440 | tf_op jit(solution)/shard_map/ppermute | solution.py:207
  212.7 4.5 %collective-permute-done.8 = f32[1,1536]{1,0:T(1,128)S(1)} collective-permute-done((f32[1,1536]{1,0:T(1,128)S(1)}, f32[1,1536]{1,0:T(1,128)S(1)}, u32[]{:S(2)}, u32[]{:S(2)}) %collective-permute-start.8) | collective-permute-done | bytes 6176 | tf_op jit(solution)/shard_map/ppermute | solution.py:207
  217.2 0.6 add.68
  (13 shorter events, 0.1 us)
Async XLA Ops:
  7.2 110.3 %all-gather.2.cloned.1.call-start = ((), (), s32[]{:S(2)}) async-start(), calls=%async_computation | async-start | bytes 19169280 | tf_op jit(solution)/shard_map/all_gather | solution.py:169
  117.6 6.1 %copy-start.1 = (f32[1,1536]{1,0:T(1,128)S(1)}, f32[1,1536]{1,0:T(1,128)}, u32[]{:S(2)}) copy-start(f32[1,1536]{1,0:T(1,128)} %param.17) | copy-start | bytes 18436
  117.7 6.0 %collective-permute-start = (bf16[128,1536]{1,0:T(8,128)(2,1)S(1)}, bf16[128,1536]{1,0:T(8,128)(2,1)S(1)}, u32[]{:S(2)}, u32[]{:S(2)}) collective-permute-start(bf16[128,1536]{1,0:T(8,128)(2,1)S(1)} %get-tuple-element.111), channel_id=1, source_target_pairs={{192,128},{193,129},{194,130},{195,131},{196,132},{197,133},{198,1... | collective-permute-start | bytes 1179656 | tf_op jit(solution)/shard_map/ppermute | solution.py:202
  123.7 0.7 collective-permute-start.1
  124.4 56.7 %copy-start = (bf16[128,1536]{1,0:T(8,128)(2,1)}, bf16[128,1536]{1,0:T(8,128)(2,1)S(1)}, u32[]{:S(2)}) copy-start(bf16[128,1536]{1,0:T(8,128)(2,1)S(1)} %get-tuple-element.114) | copy-start | bytes 1179652
  124.5 56.6 %collective-permute-start.2 = (bf16[128,1536]{1,0:T(8,128)(2,1)S(1)}, bf16[128,1536]{1,0:T(8,128)(2,1)S(1)}, u32[]{:S(2)}, u32[]{:S(2)}) collective-permute-start(bf16[128,1536]{1,0:T(8,128)(2,1)S(1)} %get-tuple-element.114), channel_id=1, source_target_pairs={{64,0},{65,1},{66,2},{67,3},{68,4},{69,5},{70,6},{71,7},{72,8},{73... | collective-permute-start | bytes 1179656 | tf_op jit(solution)/shard_map/ppermute | solution.py:202
  191.1 1.2 collective-permute-start.3
  192.3 3.7 %collective-permute-start.4 = (f32[1,1536]{1,0:T(1,128)S(1)}, f32[1,1536]{1,0:T(1,128)S(1)}, u32[]{:S(2)}, u32[]{:S(2)}) collective-permute-start(f32[1,1536]{1,0:T(1,128)S(1)} %add.63), channel_id=1, source_target_pairs={{0,2},{2,0},{4,6},{6,4},{1,3},{3,1},{5,7},{7,5},{8,10},{10,8},{12,... | collective-permute-start | bytes 18440 | tf_op jit(solution)/shard_map/ppermute | solution.py:205
  196.0 5.2 %collective-permute-start.5 = (f32[1,1536]{1,0:T(1,128)S(1)}, f32[1,1536]{1,0:T(1,128)S(1)}, u32[]{:S(2)}, u32[]{:S(2)}) collective-permute-start(f32[1,1536]{1,0:T(1,128)S(1)} %add.64), channel_id=1, source_target_pairs={{0,4},{2,6},{4,0},{6,2},{1,5},{3,7},{5,1},{7,3},{8,12},{10,14},{12... | collective-permute-start | bytes 18440 | tf_op jit(solution)/shard_map/ppermute | solution.py:205
  201.2 3.7 %collective-permute-start.6 = (f32[1,1536]{1,0:T(1,128)S(1)}, f32[1,1536]{1,0:T(1,128)S(1)}, u32[]{:S(2)}, u32[]{:S(2)}) collective-permute-start(f32[1,1536]{1,0:T(1,128)S(1)} %add.65), channel_id=1, source_target_pairs={{0,8},{8,0},{16,24},{24,16},{32,40},{40,32},{48,56},{56,48},{1,9},... | collective-permute-start | bytes 18440 | tf_op jit(solution)/shard_map/ppermute | solution.py:207
  204.9 4.6 %collective-permute-start.7 = (f32[1,1536]{1,0:T(1,128)S(1)}, f32[1,1536]{1,0:T(1,128)S(1)}, u32[]{:S(2)}, u32[]{:S(2)}) collective-permute-start(f32[1,1536]{1,0:T(1,128)S(1)} %add.66), channel_id=1, source_target_pairs={{0,16},{8,24},{16,0},{24,8},{32,48},{40,56},{48,32},{56,40},{1,17}... | collective-permute-start | bytes 18440 | tf_op jit(solution)/shard_map/ppermute | solution.py:207
  209.6 7.6 %collective-permute-start.8 = (f32[1,1536]{1,0:T(1,128)S(1)}, f32[1,1536]{1,0:T(1,128)S(1)}, u32[]{:S(2)}, u32[]{:S(2)}) collective-permute-start(f32[1,1536]{1,0:T(1,128)S(1)} %add.67), channel_id=1, source_target_pairs={{0,32},{8,40},{16,48},{24,56},{32,0},{40,8},{48,16},{56,24},{1,33}... | collective-permute-start | bytes 18440 | tf_op jit(solution)/shard_map/ppermute | solution.py:207
Sparse Core Ops, SparseCore 0:
  11.3 106.1 all-gather.1
